TPU v7x, 256 devices: a whole 4x4x8 slice. The times are simulated.
256 devices in a mesh: dp: 8 (over x, core), expert: 32 (over z, y).
Axes of the slice: x: 4, y: 4, z: 8, core: 2. Of those that a mesh axis runs over, the one named last changes fastest.
Arguments:
- tokens: bfloat16 [12288, 2048], P(('dp', 'expert')), may hold values from -6 to 6
- grad_out: bfloat16 [12288, 2048], P(('dp', 'expert')), may hold values from -6 to 6
- expert_ids: int32 [12288, 8], P(('dp', 'expert')), may hold values from 0 to 31, all different within a row; in each aligned block of 48 rows (0 to 47, 48 to 95, ...) at most 13 rows name the same one
- combine: float32 [12288, 8], P(('dp', 'expert')), may hold values from 0.03 to 0.5
- w_gate: bfloat16 [32, 2048, 768], P('expert'), may hold values from -0.125 to 0.125
- w_up: bfloat16 [32, 2048, 768], P('expert'), may hold values from -0.125 to 0.125
- w_down: bfloat16 [32, 768, 2048], P('expert'), may hold values from -0.21875 to 0.21875
- dither_keys: int32 [2], replicated, may hold values from 0 to 999999999
Outputs:
- grad_tokens: bfloat16 [12288, 2048], P(('dp', 'expert'))
- grad_combine: bfloat16 [12288, 8], P(('dp', 'expert'))
- grad_gate: bfloat16 [32, 2048, 768], P('expert', 'dp')
- grad_up: bfloat16 [32, 2048, 768], P('expert', 'dp')
- grad_down: bfloat16 [32, 768, 2048], P('expert', None, 'dp')
Inputs may be any that keep to these rules, and one draw needn't show every extreme that they name: `expert_ids`: in the rows of one device no expert is named more than 13 times, a bound that some block reaches; the 8 experts of a token differ; every expert is named somewhere.
All inputs are finite; a program needn't handle non-finite values.
Results may differ from a plain program's by a relative error of at most 0.017.
Values may be sent and summed in bfloat16 or wider, within the bound.
No kernel may reach another device: no remote copies, remote signals or barrier semaphores. Data moves between devices by JAX's collectives and lax.ppermute only.
A program may use at most 128 MiB of HBM per device.

v0:
```python
import jax
import jax.numpy as jnp
from jax import lax
from jax.sharding import PartitionSpec as P


def mix_bits(hashed):
    hashed = jnp.bitwise_xor(hashed, jnp.bitwise_and(jnp.right_shift(hashed, 16), 65535))
    hashed = hashed * 2146121005
    hashed = jnp.bitwise_xor(hashed, jnp.bitwise_and(jnp.right_shift(hashed, 15), 131071))
    hashed = hashed * 1284865837
    hashed = jnp.bitwise_xor(hashed, jnp.bitwise_and(jnp.right_shift(hashed, 16), 65535))
    return hashed


def dither(row_block, tok_index, key_word):
    columns = jnp.arange(row_block.shape[1], dtype=jnp.int32)
    salted = mix_bits(key_word + 977)
    keyed_hash = mix_bits(jnp.bitwise_xor(tok_index[:, None] * 4099 + columns[None, :], salted))
    uniform_val = jnp.bitwise_and(keyed_hash, 65535).astype(jnp.float32) * (1.0 / 65536.0)
    values = row_block.astype(jnp.float32)
    magnitude = jnp.abs(values)
    spacing = jnp.full(magnitude.shape, 2.0 ** (-9), jnp.float32)
    for power in range(-5, 9):
        spacing = jnp.where(magnitude >= 2.0**power, spacing * 2.0, spacing)
    rounded = jnp.floor(magnitude / spacing + uniform_val) * spacing
    return jnp.where(values < 0, -rounded, rounded).astype(jnp.bfloat16)


def send_rows(gate_rows_grad, up_rows_grad, gate_w, up_w, comb_slot, owners, capacity):
    row_grad = (
        jnp.dot(gate_rows_grad, gate_w.T, preferred_element_type=jnp.float32)
        + jnp.dot(up_rows_grad, up_w.T, preferred_element_type=jnp.float32)
    ).astype(jnp.bfloat16)
    return (
        lax.all_to_all(
            row_grad.reshape(owners, capacity, row_grad.shape[1]),
            "expert",
            split_axis=0,
            concat_axis=0,
            tiled=True,
        ),
        lax.all_to_all(
            comb_slot.reshape(owners, capacity), "expert", split_axis=0, concat_axis=0, tiled=True
        ),
    )


def body(tokens, grad_out, expert_ids, combine, w_gate, w_up, w_down, dither_keys):
    tok_dev, model_width = tokens.shape
    fan_out = expert_ids.shape[1]
    owners = lax.axis_size("expert")
    capacity = 9 * tok_dev * fan_out // (8 * owners)
    slot_count = owners * capacity
    source_block = lax.axis_index("dp") * owners + lax.axis_index("expert")
    tok_index = source_block * tok_dev + jnp.arange(tok_dev, dtype=jnp.int32)
    x_dith = dither(tokens, tok_index, dither_keys[0])
    g_dith = dither(grad_out, tok_index, dither_keys[1])
    flat_ids = expert_ids.reshape(-1)
    onehot = (flat_ids[:, None] == jnp.arange(owners, dtype=jnp.int32)[None, :]).astype(jnp.int32)
    position = jnp.sum((jnp.cumsum(onehot, axis=0) - 1) * onehot, axis=1)
    slot_index = flat_ids * capacity + position
    pair_rows = jnp.arange(tok_dev * fan_out, dtype=jnp.int32)
    source_row = (
        jnp.full((slot_count,), tok_dev, jnp.int32).at[slot_index].set(pair_rows // fan_out)
    )
    slot_weight = (
        jnp.zeros((slot_count,), jnp.bfloat16)
        .at[slot_index]
        .set(combine.reshape(-1).astype(jnp.bfloat16))
    )
    empty_row = jnp.zeros((1, model_width), jnp.bfloat16)
    x_send = jnp.concatenate([x_dith, empty_row], axis=0)[source_row].reshape(
        owners, capacity, model_width
    )
    g_send = jnp.concatenate([g_dith, empty_row], axis=0)[source_row].reshape(
        owners, capacity, model_width
    )
    x_recv, g_recv, w_recv = (
        lax.all_to_all(x_send, "expert", split_axis=0, concat_axis=0, tiled=True),
        lax.all_to_all(g_send, "expert", split_axis=0, concat_axis=0, tiled=True),
        lax.all_to_all(
            slot_weight.reshape(owners, capacity), "expert", split_axis=0, concat_axis=0, tiled=True
        ),
    )
    row_x = x_recv.reshape(slot_count, model_width)
    row_g = g_recv.reshape(slot_count, model_width)
    weight = w_recv.reshape(slot_count, 1).astype(jnp.float32)
    gate_w = w_gate[0]
    up_w = w_up[0]
    down_w = w_down[0]
    gate_pre = jnp.dot(row_x, gate_w, preferred_element_type=jnp.float32)
    up_pre = jnp.dot(row_x, up_w, preferred_element_type=jnp.float32)
    sigmoid_val = jax.nn.sigmoid(gate_pre)
    silu_val = gate_pre * sigmoid_val
    hidden = (silu_val * up_pre).astype(jnp.bfloat16)
    back_grad = jnp.dot(row_g, down_w.T, preferred_element_type=jnp.float32)
    comb_slot = jnp.sum(hidden.astype(jnp.float32) * back_grad, axis=1).astype(jnp.bfloat16)
    hidden_grad = weight * back_grad
    gate_rows_grad = (
        hidden_grad * up_pre * sigmoid_val * (1.0 + gate_pre * (1.0 - sigmoid_val))
    ).astype(jnp.bfloat16)
    up_rows_grad = (hidden_grad * silu_val).astype(jnp.bfloat16)
    scaled_grad = (weight * row_g.astype(jnp.float32)).astype(jnp.bfloat16)
    back_rows, back_comb = send_rows(
        gate_rows_grad, up_rows_grad, gate_w, up_w, comb_slot, owners, capacity
    )
    gate_part = jnp.dot(row_x.T, gate_rows_grad, preferred_element_type=jnp.float32)
    up_part = jnp.dot(row_x.T, up_rows_grad, preferred_element_type=jnp.float32)
    down_part = jnp.dot(hidden.T, scaled_grad, preferred_element_type=jnp.float32)
    gate_grad, up_grad, down_grad = (
        lax.psum_scatter(
            gate_part.astype(jnp.bfloat16), "dp", scatter_dimension=0, tiled=True
        ).astype(jnp.float32),
        lax.psum_scatter(
            up_part.astype(jnp.bfloat16), "dp", scatter_dimension=0, tiled=True
        ).astype(jnp.float32),
        lax.psum_scatter(
            down_part.astype(jnp.bfloat16), "dp", scatter_dimension=1, tiled=True
        ).astype(jnp.float32),
    )
    back_flat = back_rows.reshape(slot_count, model_width)[slot_index]
    grad_tokens = jnp.sum(
        back_flat.reshape(tok_dev, fan_out, model_width).astype(jnp.float32), axis=1
    ).astype(jnp.bfloat16)
    grad_combine = back_comb.reshape(slot_count)[slot_index].reshape(tok_dev, fan_out)
    return (
        grad_tokens,
        grad_combine,
        gate_grad.astype(jnp.bfloat16)[None],
        up_grad.astype(jnp.bfloat16)[None],
        down_grad.astype(jnp.bfloat16)[None],
    )


def solution(mesh):
    return jax.shard_map(
        body,
        mesh=mesh,
        in_specs=(
            P(("dp", "expert"), None),
            P(("dp", "expert"), None),
            P(("dp", "expert"), None),
            P(("dp", "expert"), None),
            P("expert", None, None),
            P("expert", None, None),
            P("expert", None, None),
            P(),
        ),
        out_specs=(
            P(("dp", "expert"), None),
            P(("dp", "expert"), None),
            P("expert", "dp", None),
            P("expert", "dp", None),
            P("expert", None, "dp"),
        ),
        check_vma=False,
    )
```

profile of v0, /device:TPU:8, one launch (start us, length us, event | category | flops | bytes accessed | tf_op | source)
XLA Modules:
  0.0 293.4 jit_solution(14848178760171916307)
XLA Ops:
  11.4 3.0 %scatter_custom_fusion = bf16[416]{0:T(512)(128)(2,1)S(1)} fusion(s32[384]{0:T(512)S(1)} %fusion.58, bf16[384]{0:T(512)(128)(2,1)S(1)} %reshape.175, bf16[]{:T(256)} %constant.40.clone.1), kind=kCustom, calls=%fused_computation.125 | custom fusion | bytes 834 | tf_op jit(solution)/shard_map/scatter | solution.py:70
  15.1 11.7 %all-to-all-start = ((bf16[32,1,13]{2,1,0:T(2,128)(2,1)}), bf16[32,1,13]{2,1,0:T(2,128)(2,1)S(1)}, u32[]{:S(2)}, u32[]{:S(2)}) async-start(bf16[32,1,13]{2,1,0:T(2,128)(2,1)} %all_to_all.25), calls=%async_computation | async-start | bytes 32768 | tf_op jit(solution)/shard_map/all_to_all | solution.py:82
  29.5 2.9 scatter_custom_fusion.1
  32.4 3.3 %fusion.50 = (bf16[48,2048]{1,0:T(8,128)(2,1)}, bf16[48,2048]{1,0:T(8,128)(2,1)S(1)}) fusion(bf16[48,2048]{1,0:T(8,128)(2,1)} %param.9, s32[]{:T(128)S(6)} %xor.50, s32[48]{0:T(128)S(1)} %add_multiply_fusion, s32[]{:T(128)S(6)} %xor.58, bf16[48,2048]{1,0:T(8,128)(2,1)} %param.8), kind=kLoop, calls=%fused_computation.98 | loop fusion | flops 13074432 | bytes 786632 | tf_op jit(solution)/shard_map/convert_element_type | solution.py:27
  35.8 3.2 %gather_fusion.1 = bf16[416,2048]{1,0:T(8,128)(2,1)} fusion(bf16[49,2048]{1,0:T(8,128)(2,1)S(1)} %concatenate.7, s32[1024]{0:T(1024)S(1)} %pad_clamp_fusion.1), kind=kCustom, calls=%fused_computation.1 | custom fusion | bytes 3409536 | tf_op jit(solution)/shard_map/gather | solution.py:73
  41.7 9.8 %all-to-all-start.2 = ((bf16[32,13,2048]{2,1,0:T(8,128)(2,1)}), bf16[32,13,2048]{2,1,0:T(8,128)(2,1)}, u32[]{:S(2)}, u32[]{:S(2)}) async-start(bf16[32,13,2048]{2,1,0:T(8,128)(2,1)} %reshape.131), calls=%async_computation.2 | async-start | bytes 4194304 | tf_op jit(solution)/shard_map/all_to_all | solution.py:80
  52.5 3.1 %gather_fusion = bf16[416,2048]{1,0:T(8,128)(2,1)} fusion(bf16[49,2048]{1,0:T(8,128)(2,1)S(1)} %concatenate.6, s32[1024]{0:T(1024)S(1)} %pad_clamp_fusion.1), kind=kCustom, calls=%fused_computation | custom fusion | bytes 3409536 | tf_op jit(solution)/shard_map/gather | solution.py:76
  55.6 2.8 reshape.129
  58.4 42.0 %all-to-all-done.2 = bf16[32,13,2048]{2,1,0:T(8,128)(2,1)} async-done(((bf16[32,13,2048]{2,1,0:T(8,128)(2,1)}), bf16[32,13,2048]{2,1,0:T(8,128)(2,1)}, u32[]{:S(2)}, u32[]{:S(2)}) %all-to-all-start.2) | async-done | bytes 1703968 | tf_op jit(solution)/shard_map/all_to_all | solution.py:80
  100.4 6.8 %all-to-all-start.1 = ((bf16[32,13,2048]{2,1,0:T(8,128)(2,1)}), bf16[32,13,2048]{2,1,0:T(8,128)(2,1)}, u32[]{:S(2)}, u32[]{:S(2)}) async-start(bf16[32,13,2048]{2,1,0:T(8,128)(2,1)} %reshape.129), calls=%async_computation.1 | async-start | bytes 4194304 | tf_op jit(solution)/shard_map/all_to_all | solution.py:81
  110.4 4.2 %fusion.2 = f32[416,768]{1,0:T(8,128)} fusion(bf16[416,2048]{1,0:T(8,128)(2,1)} %reshape.132, bf16[1,2048,768]{2,1,0:T(8,128)(2,1)S(1)} %copy-done), kind=kOutput, calls=%fused_computation.13 | convolution fusion | flops 1308622848 | bytes 6127616 | tf_op jit(solution)/shard_map/dot_general | solution.py:92
  117.1 39.3 %all-to-all-done.1 = bf16[32,13,2048]{2,1,0:T(8,128)(2,1)} async-done(((bf16[32,13,2048]{2,1,0:T(8,128)(2,1)}), bf16[32,13,2048]{2,1,0:T(8,128)(2,1)}, u32[]{:S(2)}, u32[]{:S(2)}) %all-to-all-start.1) | async-done | bytes 1703968 | tf_op jit(solution)/shard_map/all_to_all | solution.py:81
  159.1 6.3 %multiply_reduce_fusion = (bf16[416]{0:T(512)(128)(2,1)S(1)}, bf16[416,768]{1,0:T(8,128)(2,1)S(1)}, bf16[416,768]{1,0:T(8,128)(2,1)}, bf16[416,768]{1,0:T(8,128)(2,1)}) fusion(f32[416,768]{1,0:T(8,128)} %fusion.6, f32[416,768]{1,0:T(8,128)} %fusion.2, f32[416]{0:T(512)S(1)} %reshape.138, bf16[416,2048]{1,0:T(8,128)(2,1)} %reshape.130, ...), kind=kOutput, calls=%fused_computation.23 | convolution fusion | flops 1314692736 | bytes 9324992 | tf_op jit(solution)/shard_map/dot_general | solution.py:97
  165.4 3.6 %convolution_convert_fusion = bf16[768,2048]{1,0:T(8,128)(2,1)} fusion(bf16[416,768]{1,0:T(8,128)(2,1)S(1)} %get-tuple-element.16, bf16[416,2048]{1,0:T(8,128)(2,1)S(1)} %copy-done.2, f32[416]{0:T(512)S(1)} %reshape.138), kind=kOutput, calls=%fused_computation.8 | convolution fusion | flops 1312751616 | bytes 5490304 | tf_op jit(solution)/shard_map/dot_general | solution.py:110
  169.1 5.1 %convolution_convert_fusion.2 = bf16[2048,768]{1,0:T(8,128)(2,1)} fusion(bf16[416,2048]{1,0:T(8,128)(2,1)} %reshape.132, bf16[416,768]{1,0:T(8,128)(2,1)} %get-tuple-element.17), kind=kOutput, calls=%fused_computation.10 | convolution fusion | flops 1310195712 | bytes 5488640 | tf_op jit(solution)/shard_map/dot_general | solution.py:108
  174.3 5.1 %convolution_convert_fusion.1 = bf16[2048,768]{1,0:T(8,128)(2,1)} fusion(bf16[416,2048]{1,0:T(8,128)(2,1)} %reshape.132, bf16[416,768]{1,0:T(8,128)(2,1)} %get-tuple-element.18), kind=kOutput, calls=%fused_computation.9 | convolution fusion | flops 1310195712 | bytes 5488640 | tf_op jit(solution)/shard_map/dot_general | solution.py:109
  180.2 5.6 %all-to-all-start.4 = ((bf16[32,1,13]{2,1,0:T(2,128)(2,1)}), bf16[32,1,13]{2,1,0:T(2,128)(2,1)S(1)}, u32[]{:S(2)}, u32[]{:S(2)}) async-start(bf16[32,1,13]{2,1,0:T(2,128)(2,1)} %convert_element_type.116), calls=%async_computation.4 | async-start | bytes 32768 | tf_op jit(solution)/shard_map/all_to_all | solution.py:43
  191.3 2.9 reshape.133
  194.3 9.8 %all-to-all-start.3 = ((bf16[32,13,2048]{2,1,0:T(8,128)(2,1)}), bf16[32,13,2048]{2,1,0:T(8,128)(2,1)}, u32[]{:S(2)}, u32[]{:S(2)}) async-start(bf16[32,13,2048]{2,1,0:T(8,128)(2,1)} %reshape.133), calls=%async_computation.3 | async-start | bytes 4194304 | tf_op jit(solution)/shard_map/all_to_all | solution.py:36
  204.2 2.8 gather_fusion.3
  207.8 43.2 %all-to-all-done.3 = bf16[32,13,2048]{2,1,0:T(8,128)(2,1)} async-done(((bf16[32,13,2048]{2,1,0:T(8,128)(2,1)}), bf16[32,13,2048]{2,1,0:T(8,128)(2,1)}, u32[]{:S(2)}, u32[]{:S(2)}) %all-to-all-start.3) | async-done | bytes 1703968 | tf_op jit(solution)/shard_map/all_to_all | solution.py:36
  253.7 6.8 %gather_fusion.2 = bf16[384,2048]{1,0:T(8,128)(2,1)} fusion(bf16[416,2048]{1,0:T(8,128)(2,1)} %reshape.134, s32[1024]{0:T(1024)S(1)} %pad_clamp_fusion), kind=kCustom, calls=%fused_computation.2 | custom fusion | bytes 3147264 | tf_op jit(solution)/shard_map/gather | solution.py:122
  260.5 3.2 %bitcast_reduce_fusion = bf16[48,2048]{1,0:T(8,128)(2,1)} fusion(bf16[384,2048]{1,0:T(8,128)(2,1)} %gather_fusion.2), kind=kLoop, calls=%fused_computation.22 | loop fusion | flops 688128 | bytes 1769472 | tf_op jit(solution)/shard_map/reduce_sum | solution.py:123
  263.7 23.2 %reduce-scatter.6.cloned.1.call-done = bf16[256,768]{1,0:T(8,128)(2,1)} async-done(((bf16[2048,768]{1,0:T(8,128)(2,1)}), bf16[256,768]{1,0:T(8,128)(2,1)}) %reduce-scatter.6.cloned.1.call-update) | async-done | bytes 393232 | tf_op jit(solution)/shard_map/reduce_scatter | solution.py:115
  (60 shorter events, 28.6 us)
Async XLA Ops:
  7.2 103.2 %copy-start = (bf16[1,2048,768]{2,1,0:T(8,128)(2,1)S(1)}, bf16[1,2048,768]{2,1,0:T(8,128)(2,1)}, u32[]{:S(2)}) copy-start(bf16[1,2048,768]{2,1,0:T(8,128)(2,1)} %param.12) | copy-start | bytes 9437188
  15.1 26.6 %all-to-all-start = ((bf16[32,1,13]{2,1,0:T(2,128)(2,1)}), bf16[32,1,13]{2,1,0:T(2,128)(2,1)S(1)}, u32[]{:S(2)}, u32[]{:S(2)}) async-start(bf16[32,1,13]{2,1,0:T(2,128)(2,1)} %all_to_all.25), calls=%async_computation | async-start | bytes 32768 | tf_op jit(solution)/shard_map/all_to_all | solution.py:82
  41.7 58.7 %all-to-all-start.2 = ((bf16[32,13,2048]{2,1,0:T(8,128)(2,1)}), bf16[32,13,2048]{2,1,0:T(8,128)(2,1)}, u32[]{:S(2)}, u32[]{:S(2)}) async-start(bf16[32,13,2048]{2,1,0:T(8,128)(2,1)} %reshape.131), calls=%async_computation.2 | async-start | bytes 4194304 | tf_op jit(solution)/shard_map/all_to_all | solution.py:80
  100.4 56.0 %all-to-all-start.1 = ((bf16[32,13,2048]{2,1,0:T(8,128)(2,1)}), bf16[32,13,2048]{2,1,0:T(8,128)(2,1)}, u32[]{:S(2)}, u32[]{:S(2)}) async-start(bf16[32,13,2048]{2,1,0:T(8,128)(2,1)} %reshape.129), calls=%async_computation.1 | async-start | bytes 4194304 | tf_op jit(solution)/shard_map/all_to_all | solution.py:81
  107.2 156.5 %reduce-scatter.8.cloned.1.call-start = ((), (), s32[]{:S(2)}) async-start(), calls=%async_computation.10 | async-start | bytes 3538944 | tf_op jit(solution)/shard_map/reduce_scatter | solution.py:118
  110.4 4.2 %copy-start.1 = (bf16[416,2048]{1,0:T(8,128)(2,1)S(1)}, bf16[416,2048]{1,0:T(8,128)(2,1)}, u32[]{:S(2)}) copy-start(bf16[416,2048]{1,0:T(8,128)(2,1)} %reshape.132) | copy-start | bytes 5111812
  110.4 4.2 %copy-start.3 = (bf16[1,2048,768]{2,1,0:T(8,128)(2,1)S(1)}, bf16[1,2048,768]{2,1,0:T(8,128)(2,1)}, u32[]{:S(2)}) copy-start(bf16[1,2048,768]{2,1,0:T(8,128)(2,1)} %param.13) | copy-start | bytes 9437188
  159.1 6.3 %copy-start.2 = (bf16[416,2048]{1,0:T(8,128)(2,1)S(1)}, bf16[416,2048]{1,0:T(8,128)(2,1)}, u32[]{:S(2)}) copy-start(bf16[416,2048]{1,0:T(8,128)(2,1)} %reshape.130) | copy-start | bytes 5111812
  169.1 94.6 %reduce-scatter.4.cloned.1.call-start = ((), (), s32[]{:S(2)}) async-start(), calls=%async_computation.8 | async-start | bytes 3538944 | tf_op jit(solution)/shard_map/reduce_scatter | solution.py:112
  174.3 112.6 %reduce-scatter.6.cloned.1.call-start = ((), (), s32[]{:S(2)}) async-start(), calls=%async_computation.9 | async-start | bytes 3538944 | tf_op jit(solution)/shard_map/reduce_scatter | solution.py:115
  180.2 14.1 %all-to-all-start.4 = ((bf16[32,1,13]{2,1,0:T(2,128)(2,1)}), bf16[32,1,13]{2,1,0:T(2,128)(2,1)S(1)}, u32[]{:S(2)}, u32[]{:S(2)}) async-start(bf16[32,1,13]{2,1,0:T(2,128)(2,1)} %convert_element_type.116), calls=%async_computation.4 | async-start | bytes 32768 | tf_op jit(solution)/shard_map/all_to_all | solution.py:43
  185.8 2.8 copy-start.4
  185.8 2.8 copy-start.5
  194.3 56.7 %all-to-all-start.3 = ((bf16[32,13,2048]{2,1,0:T(8,128)(2,1)}), bf16[32,13,2048]{2,1,0:T(8,128)(2,1)}, u32[]{:S(2)}, u32[]{:S(2)}) async-start(bf16[32,13,2048]{2,1,0:T(8,128)(2,1)} %reshape.133), calls=%async_computation.3 | async-start | bytes 4194304 | tf_op jit(solution)/shard_map/all_to_all | solution.py:36
Sparse Core Ops, SparseCore 0:
  169.2 35.3 reduce-scatter.7
  207.7 38.2 reduce-scatter.3
  249.2 37.5 reduce-scatter.5
where the time goes:
time: 294 us; the launch traced here: 293 us
  waiting for transfers between devices  148 us (50%)
  local copies, waits for them, and re-layouts  44.8 us (15%)
  starting transfers between devices  44 us (15%)
  matrix products  32.4 us (11%)
  between operations  15.3 us (5%)
  other arithmetic  9.21 us (3%)
    all_to_all x1, waiting for transfers between devices, send_rows(): lax.all_to_all(row_grad.reshape(owners, capacity, row_grad.shape[1]), 'ex...  43.2 us
    all_to_all x1, waiting for transfers between devices, body(): lax.all_to_all(x_send, 'expert', split_axis=0, concat_axis=0, tiled=True)  42 us
    all_to_all x1, waiting for transfers between devices, body(): lax.all_to_all(g_send, 'expert', split_axis=0, concat_axis=0, tiled=True)  39.3 us
    reduce_scatter x1, waiting for transfers between devices, body(): lax.psum_scatter(up_part.astype(jnp.bfloat16), 'dp', scatter_dimension=0,...  23.2 us
    all_to_all x1, starting transfers between devices, body(): lax.all_to_all(slot_weight.reshape(owners, capacity), 'expert', split_axi...  11.7 us
    all_to_all x1, starting transfers between devices, body(): lax.all_to_all(x_send, 'expert', split_axis=0, concat_axis=0, tiled=True)  9.83 us
    all_to_all x1, starting transfers between devices, send_rows(): lax.all_to_all(row_grad.reshape(owners, capacity, row_grad.shape[1]), 'ex...  9.76 us
    all_to_all x1, starting transfers between devices, body(): lax.all_to_all(g_send, 'expert', split_axis=0, concat_axis=0, tiled=True)  6.81 us
  transfers between devices with their start and end apart: 8, of which 5 were waited for; matrix products, arithmetic and copies ran while one was open for 22% of the time, Pallas kernels for 0%

commit v1 on v0

--- a/solution.py
+++ b/solution.py
@@ -27,31 +27,13 @@
     return jnp.where(values < 0, -rounded, rounded).astype(jnp.bfloat16)
 
 
-def send_rows(gate_rows_grad, up_rows_grad, gate_w, up_w, comb_slot, owners, capacity):
-    row_grad = (
-        jnp.dot(gate_rows_grad, gate_w.T, preferred_element_type=jnp.float32)
-        + jnp.dot(up_rows_grad, up_w.T, preferred_element_type=jnp.float32)
-    ).astype(jnp.bfloat16)
-    return (
-        lax.all_to_all(
-            row_grad.reshape(owners, capacity, row_grad.shape[1]),
-            "expert",
-            split_axis=0,
-            concat_axis=0,
-            tiled=True,
-        ),
-        lax.all_to_all(
-            comb_slot.reshape(owners, capacity), "expert", split_axis=0, concat_axis=0, tiled=True
-        ),
-    )
-
-
 def body(tokens, grad_out, expert_ids, combine, w_gate, w_up, w_down, dither_keys):
     tok_dev, model_width = tokens.shape
     fan_out = expert_ids.shape[1]
     owners = lax.axis_size("expert")
     capacity = 9 * tok_dev * fan_out // (8 * owners)
     slot_count = owners * capacity
+    lane = 128
     source_block = lax.axis_index("dp") * owners + lax.axis_index("expert")
     tok_index = source_block * tok_dev + jnp.arange(tok_dev, dtype=jnp.int32)
     x_dith = dither(tokens, tok_index, dither_keys[0])
@@ -69,23 +51,21 @@
         .at[slot_index]
         .set(combine.reshape(-1).astype(jnp.bfloat16))
     )
-    empty_row = jnp.zeros((1, model_width), jnp.bfloat16)
-    x_send = jnp.concatenate([x_dith, empty_row], axis=0)[source_row].reshape(
-        owners, capacity, model_width
+    token_table = jnp.concatenate(
+        [
+            jnp.concatenate([x_dith, g_dith], axis=1),
+            jnp.zeros((1, 2 * model_width), jnp.bfloat16),
+        ],
+        axis=0,
     )
-    g_send = jnp.concatenate([g_dith, empty_row], axis=0)[source_row].reshape(
-        owners, capacity, model_width
-    )
-    x_recv, g_recv, w_recv = (
-        lax.all_to_all(x_send, "expert", split_axis=0, concat_axis=0, tiled=True),
-        lax.all_to_all(g_send, "expert", split_axis=0, concat_axis=0, tiled=True),
-        lax.all_to_all(
-            slot_weight.reshape(owners, capacity), "expert", split_axis=0, concat_axis=0, tiled=True
-        ),
-    )
-    row_x = x_recv.reshape(slot_count, model_width)
-    row_g = g_recv.reshape(slot_count, model_width)
-    weight = w_recv.reshape(slot_count, 1).astype(jnp.float32)
+    weight_cols = jnp.pad(slot_weight[:, None], ((0, 0), (0, lane - 1)))
+    send = jnp.concatenate([token_table[source_row], weight_cols], axis=1)
+    recv = lax.all_to_all(
+        send.reshape(owners, capacity, send.shape[1]), "expert", split_axis=0, concat_axis=0, tiled=True
+    ).reshape(slot_count, send.shape[1])
+    row_x = recv[:, :model_width]
+    row_g = recv[:, model_width : 2 * model_width]
+    weight = recv[:, 2 * model_width : 2 * model_width + 1].astype(jnp.float32)
     gate_w = w_gate[0]
     up_w = w_up[0]
     down_w = w_down[0]
@@ -102,34 +82,43 @@
     ).astype(jnp.bfloat16)
     up_rows_grad = (hidden_grad * silu_val).astype(jnp.bfloat16)
     scaled_grad = (weight * row_g.astype(jnp.float32)).astype(jnp.bfloat16)
-    back_rows, back_comb = send_rows(
-        gate_rows_grad, up_rows_grad, gate_w, up_w, comb_slot, owners, capacity
-    )
     gate_part = jnp.dot(row_x.T, gate_rows_grad, preferred_element_type=jnp.float32)
     up_part = jnp.dot(row_x.T, up_rows_grad, preferred_element_type=jnp.float32)
-    down_part = jnp.dot(hidden.T, scaled_grad, preferred_element_type=jnp.float32)
-    gate_grad, up_grad, down_grad = (
-        lax.psum_scatter(
-            gate_part.astype(jnp.bfloat16), "dp", scatter_dimension=0, tiled=True
-        ).astype(jnp.float32),
-        lax.psum_scatter(
-            up_part.astype(jnp.bfloat16), "dp", scatter_dimension=0, tiled=True
-        ).astype(jnp.float32),
-        lax.psum_scatter(
-            down_part.astype(jnp.bfloat16), "dp", scatter_dimension=1, tiled=True
-        ).astype(jnp.float32),
+    down_part_t = jnp.dot(scaled_grad.T, hidden, preferred_element_type=jnp.float32)
+    hidden_units = gate_w.shape[1]
+    parts = jnp.concatenate(
+        [gate_part.astype(jnp.bfloat16), up_part.astype(jnp.bfloat16), down_part_t.astype(jnp.bfloat16)],
+        axis=1,
     )
-    back_flat = back_rows.reshape(slot_count, model_width)[slot_index]
+    reduced = lax.psum_scatter(parts, "dp", scatter_dimension=0, tiled=True)
+    row_grad = (
+        jnp.dot(gate_rows_grad, gate_w.T, preferred_element_type=jnp.float32)
+        + jnp.dot(up_rows_grad, up_w.T, preferred_element_type=jnp.float32)
+    ).astype(jnp.bfloat16)
+    back_send = jnp.concatenate(
+        [row_grad, jnp.pad(comb_slot[:, None], ((0, 0), (0, lane - 1)))], axis=1
+    )
+    back = lax.all_to_all(
+        back_send.reshape(owners, capacity, back_send.shape[1]),
+        "expert",
+        split_axis=0,
+        concat_axis=0,
+        tiled=True,
+    ).reshape(slot_count, back_send.shape[1])
+    back_flat = back[slot_index]
     grad_tokens = jnp.sum(
-        back_flat.reshape(tok_dev, fan_out, model_width).astype(jnp.float32), axis=1
+        back_flat[:, :model_width].reshape(tok_dev, fan_out, model_width).astype(jnp.float32), axis=1
     ).astype(jnp.bfloat16)
-    grad_combine = back_comb.reshape(slot_count)[slot_index].reshape(tok_dev, fan_out)
+    grad_combine = back_flat[:, model_width].reshape(tok_dev, fan_out)
+    gate_grad = reduced[:, :hidden_units]
+    up_grad = reduced[:, hidden_units : 2 * hidden_units]
+    down_grad = reduced[:, 2 * hidden_units :].T
     return (
         grad_tokens,
         grad_combine,
-        gate_grad.astype(jnp.bfloat16)[None],
-        up_grad.astype(jnp.bfloat16)[None],
-        down_grad.astype(jnp.bfloat16)[None],
+        gate_grad[None],
+        up_grad[None],
+        down_grad[None],
     )
 
 

time: 294 us -> 271 us (0.922)
  blocking collectives: 0 us -> 110 us
  waiting for transfers between devices: 148 us -> 50.7 us
  starting transfers between devices: 44 us -> 6.84 us
  matrix products: 32.4 us -> 17.6 us
  other arithmetic: 9.21 us -> 20.1 us
  local copies, waits for them, and re-layouts: 44.8 us -> 48.5 us
    all_to_all x0 -> x1, blocking collectives: none -> 110 us  [body(): lax.all_to_all(send.reshape(owners, capacity, send.shape[1]), 'expert', s...]
    all_to_all x5 -> x1, waiting for transfers between devices: 124 us -> 50.7 us  [body(): lax.all_to_all(back_send.reshape(owners, capacity, back_send.shape[1]), '...]
    all_to_all x5 -> x1, starting transfers between devices: 43.7 us -> 6.8 us  [body(): lax.all_to_all(back_send.reshape(owners, capacity, back_send.shape[1]), '...]
    reduce_scatter x3 -> x1, waiting for transfers between devices: 23.2 us -> 0.01 us  [body(): reduced = lax.psum_scatter(parts, 'dp', scatter_dimension=0, tiled=True)]
    concatenate x0 -> x4, other arithmetic: none -> 10.7 us  [the longest x1 4.48 us: body(): jnp.concatenate([gate_part.astype(jnp.bfloat16), up_part.astype(jnp.bfloa...]
    dot_general x1, matrix products: 6.34 us -> 2.17 us  [body(): back_grad = jnp.dot(row_g, down_w.T, preferred_element_type=jnp.float32)]
    dot_general x1, matrix products: 5.14 us -> 1.85 us  [body(): up_part = jnp.dot(row_x.T, up_rows_grad, preferred_element_type=jnp.float32)]
    dot_general x1, matrix products: 5.11 us -> 1.85 us  [body(): jnp.dot(row_x.T, gate_rows_grad, preferred_element_type=jnp.float32)]
  transfers between devices with their start and end apart: 8 -> 2, of which waited for: 5 -> 1; matrix products, arithmetic and copies ran while one was open for 22% -> 9% of each run, Pallas kernels for 0% -> 0%
where the time goes in v1:
time: 271 us; the launch traced here: 270 us
  blocking collectives  110 us (41%)
  waiting for transfers between devices  50.7 us (19%)
  local copies, waits for them, and re-layouts  48.5 us (18%)
  other arithmetic  20.1 us (7%)
  matrix products  17.6 us (6%)
  between operations  15.6 us (6%)
  starting transfers between devices  6.84 us (3%)
    all_to_all x1, blocking collectives, body(): lax.all_to_all(send.reshape(owners, capacity, send.shape[1]), 'expert', s...  110 us
    all_to_all x1, waiting for transfers between devices, body(): lax.all_to_all(back_send.reshape(owners, capacity, back_send.shape[1]), '...  50.7 us
    gather x1, local copies, waits for them, and re-layouts, body(): send = jnp.concatenate([token_table[source_row], weight_cols], axis=1)  9.4 us
    gather x1, local copies, waits for them, and re-layouts, body(): back_flat = back[slot_index]  6.96 us
    all_to_all x1, starting transfers between devices, body(): lax.all_to_all(back_send.reshape(owners, capacity, back_send.shape[1]), '...  6.8 us
  transfers between devices with their start and end apart: 2, of which 1 were waited for; matrix products, arithmetic and copies ran while one was open for 9% of the time, Pallas kernels for 0%

profile of v1, /device:TPU:8, one launch (start us, length us, event | category | flops | bytes accessed | tf_op | source)
XLA Modules:
  0.0 269.7 jit_solution(16380277949380648509)
XLA Ops:
  11.4 3.0 %scatter_custom_fusion.1 = bf16[416]{0:T(512)(128)(2,1)S(1)} fusion(s32[384]{0:T(512)S(1)} %fusion.72, bf16[384]{0:T(512)(128)(2,1)S(1)} %reshape.128, bf16[]{:T(256)} %constant.39.clone.1), kind=kCustom, calls=%fused_computation.144 | custom fusion | bytes 834 | tf_op jit(solution)/shard_map/scatter | solution.py:52
  17.2 2.9 %scatter_custom_fusion = s32[416]{0:T(512)S(1)} fusion(s32[384]{0:T(512)S(1)} %fusion.72, s32[384]{0:T(512)S(1)} %add_select_fusion, s32[]{:T(128)} %constant.29.clone.1), kind=kCustom, calls=%fused_computation.142 | custom fusion | bytes 1668 | tf_op jit(solution)/shard_map/scatter | solution.py:47
  20.1 2.7 fusion.64
  23.6 9.4 %gather_fusion = bf16[416,4096]{1,0:T(8,128)(2,1)} fusion(bf16[49,4096]{1,0:T(8,128)(2,1)} %fusion.57, s32[1024]{0:T(1024)S(1)} %pad_clamp_fusion.1), kind=kCustom, calls=%fused_computation | custom fusion | bytes 6817408 | tf_op jit(solution)/shard_map/gather | solution.py:62
  33.0 4.0 %fusion.2 = bf16[416,4224]{1,0:T(8,128)(2,1)} fusion(bf16[416,1]{1,0:T(8,128)(2,1)S(1)} %broadcast_in_dim.38, bf16[416,4096]{1,0:T(8,128)(2,1)} %gather_fusion), kind=kLoop, calls=%fused_computation.9 | loop fusion | flops 10543104 | bytes 6923072 | tf_op jit(solution)/shard_map/concatenate | solution.py:62
  37.0 5.0 %reshape.94 = bf16[32,13,4224]{2,1,0:T(8,128)(2,1)} reshape(bf16[416,4224]{1,0:T(8,128)(2,1)} %fusion.2) | data formatting | bytes 7028736 | tf_op jit(solution)/shard_map/reshape | solution.py:64
  42.1 110.3 %all_to_all.10 = bf16[32,13,4224]{2,1,0:T(8,128)(2,1)} all-to-all(bf16[32,13,4224]{2,1,0:T(8,128)(2,1)} %reshape.94), channel_id=1, replica_groups=mesh['dp'=8,'expert'=32] {'expert'}, dimensions={0} | all-to-all | bytes 7028736 | tf_op jit(solution)/shard_map/all_to_all | solution.py:63
  152.4 5.0 %reshape.95 = bf16[416,4224]{1,0:T(8,128)(2,1)} reshape(bf16[32,13,4224]{2,1,0:T(8,128)(2,1)} %all_to_all.10) | data formatting | bytes 7028736 | tf_op jit(solution)/shard_map/reshape | solution.py:65
  158.5 4.0 %fusion.9 = f32[416,768]{1,0:T(8,128)S(1)} fusion(bf16[1,2048,768]{2,1,0:T(8,128)(2,1)} %param.13, bf16[416,4224]{1,0:T(8,128)(2,1)} %reshape.95), kind=kOutput, calls=%fused_computation.21 | convolution fusion | flops 1308622848 | bytes 6127616 | tf_op jit(solution)/shard_map/dot_general | solution.py:73
  164.4 2.2 multiply_reduce_fusion
  166.6 1.9 convolution_convert_fusion
  168.5 1.9 convolution_convert_fusion.1
  170.4 1.9 convolution_convert_fusion.2
  172.3 4.5 %pad_maximum_fusion = bf16[2048,2304]{0,1:T(8,128)(2,1)} fusion(bf16[2048,768]{0,1:T(8,128)(2,1)S(1)} %convolution_convert_fusion, bf16[2048,768]{0,1:T(8,128)(2,1)S(1)} %convolution_convert_fusion.1, bf16[2048,768]{0,1:T(8,128)(2,1)S(1)} %convolution_convert_fusion.2), kind=kLoop, calls=%fused_computation.4 | loop fusion | flops 28311552 | bytes 18874368 | tf_op jit(solution)/shard_map/concatenate | solution.py:89
  176.9 2.7 %fusion.3 = f32[416,2048]{1,0:T(8,128)S(1)} fusion(bf16[416,768]{1,0:T(8,128)(2,1)} %copy-done.4, bf16[1,2048,768]{2,1,0:T(8,128)(2,1)S(1)} %copy-done), kind=kOutput, calls=%fused_computation.15 | convolution fusion | flops 1308622848 | bytes 7192576 | tf_op jit(solution)/shard_map/dot_general | solution.py:95
  179.7 1.5 add_convert_fusion
  182.6 3.0 %reshape.96 = bf16[32,13,2176]{2,1,0:T(8,128)(2,1)} reshape(bf16[416,2176]{1,0:T(8,128)(2,1)} %fusion.15) | data formatting | bytes 3620864 | tf_op jit(solution)/shard_map/reshape | solution.py:102
  185.6 6.8 %all-to-all-start.1 = ((bf16[32,13,2176]{2,1,0:T(8,128)(2,1)}), bf16[32,13,2176]{2,1,0:T(8,128)(2,1)}, u32[]{:S(2)}, u32[]{:S(2)}) async-start(bf16[32,13,2176]{2,1,0:T(8,128)(2,1)} %reshape.96), calls=%async_computation.1 | async-start | bytes 4456448 | tf_op jit(solution)/shard_map/all_to_all | solution.py:101
  192.4 50.7 %all-to-all-done.1 = bf16[32,13,2176]{2,1,0:T(8,128)(2,1)} async-done(((bf16[32,13,2176]{2,1,0:T(8,128)(2,1)}), bf16[32,13,2176]{2,1,0:T(8,128)(2,1)}, u32[]{:S(2)}, u32[]{:S(2)}) %all-to-all-start.1) | async-done | bytes 1810464 | tf_op jit(solution)/shard_map/all_to_all | solution.py:101
  243.0 2.9 %reshape.97 = bf16[416,2176]{1,0:T(8,128)(2,1)} reshape(bf16[32,13,2176]{2,1,0:T(8,128)(2,1)} %all-to-all-done.1) | data formatting | bytes 3620864 | tf_op jit(solution)/shard_map/reshape | solution.py:107
  245.9 7.0 %gather_fusion.1 = bf16[384,2176]{1,0:T(8,128)(2,1)} fusion(bf16[416,2176]{1,0:T(8,128)(2,1)} %reshape.97, s32[1024]{0:T(1024)S(1)} %pad_clamp_fusion), kind=kCustom, calls=%fused_computation.1 | custom fusion | bytes 3343872 | tf_op jit(solution)/shard_map/gather | solution.py:108
  254.7 3.2 %fusion.17 = bf16[48,2048]{1,0:T(8,128)(2,1)} fusion(bf16[384,2176]{1,0:T(8,128)(2,1)} %gather_fusion.1), kind=kLoop, calls=%fused_computation.28 | loop fusion | flops 688128 | bytes 1769472 | tf_op jit(solution)/shard_map/reduce_sum | solution.py:109
  257.8 2.2 slice_bitcast_fusion.1
  260.0 1.9 copy.24
  (48 shorter events, 13.6 us)
Async XLA Ops:
  7.2 155.4 %copy-start = (bf16[1,2048,768]{2,1,0:T(8,128)(2,1)S(1)}, bf16[1,2048,768]{2,1,0:T(8,128)(2,1)}, u32[]{:S(2)}) copy-start(bf16[1,2048,768]{2,1,0:T(8,128)(2,1)} %param.12) | copy-start | bytes 9437188
  7.2 250.6 %reduce-scatter.2.cloned.1.call-start = ((), (), s32[]{:S(2)}) async-start(), calls=%async_computation.3 | async-start | bytes 10616832 | tf_op jit(solution)/shard_map/reduce_scatter | solution.py:93
  158.5 4.1 %copy-start.1 = (bf16[416,4224]{1,0:T(8,128)(2,1)S(1)}, bf16[416,4224]{1,0:T(8,128)(2,1)}, u32[]{:S(2)}) copy-start(bf16[416,4224]{1,0:T(8,128)(2,1)} %reshape.95) | copy-start | bytes 10543108
  162.5 1.9 copy-start.2
  166.6 1.9 copy-start.5
  166.6 3.8 %copy-start.4 = (bf16[416,768]{1,0:T(8,128)(2,1)}, bf16[416,768]{1,0:T(8,128)(2,1)S(1)}, u32[]{:S(2)}) copy-start(bf16[416,768]{1,0:T(8,128)(2,1)S(1)} %get-tuple-element.17) | copy-start | bytes 1916932
  176.9 2.8 %copy-start.3 = (bf16[1,2048,768]{2,1,0:T(8,128)(2,1)S(1)}, bf16[1,2048,768]{2,1,0:T(8,128)(2,1)}, u32[]{:S(2)}) copy-start(bf16[1,2048,768]{2,1,0:T(8,128)(2,1)} %param.13) | copy-start | bytes 9437188
  176.9 2.8 %copy-start.6 = (bf16[416,768]{1,0:T(8,128)(2,1)S(1)}, bf16[416,768]{1,0:T(8,128)(2,1)}, u32[]{:S(2)}) copy-start(bf16[416,768]{1,0:T(8,128)(2,1)} %copy-done.5) | copy-start | bytes 1916932
  185.6 57.5 %all-to-all-start.1 = ((bf16[32,13,2176]{2,1,0:T(8,128)(2,1)}), bf16[32,13,2176]{2,1,0:T(8,128)(2,1)}, u32[]{:S(2)}, u32[]{:S(2)}) async-start(bf16[32,13,2176]{2,1,0:T(8,128)(2,1)} %reshape.96), calls=%async_computation.1 | async-start | bytes 4456448 | tf_op jit(solution)/shard_map/all_to_all | solution.py:101
Sparse Core Ops, SparseCore 0:
  176.9 56.4 reduce-scatter.1

commit v2 on v1

--- a/solution.py
+++ b/solution.py
@@ -33,7 +33,8 @@
     owners = lax.axis_size("expert")
     capacity = 9 * tok_dev * fan_out // (8 * owners)
     slot_count = owners * capacity
-    lane = 128
+    lanes = 128
+    tile_rows = model_width // lanes
     source_block = lax.axis_index("dp") * owners + lax.axis_index("expert")
     tok_index = source_block * tok_dev + jnp.arange(tok_dev, dtype=jnp.int32)
     x_dith = dither(tokens, tok_index, dither_keys[0])
@@ -43,29 +44,39 @@
     position = jnp.sum((jnp.cumsum(onehot, axis=0) - 1) * onehot, axis=1)
     slot_index = flat_ids * capacity + position
     pair_rows = jnp.arange(tok_dev * fan_out, dtype=jnp.int32)
-    source_row = (
-        jnp.full((slot_count,), tok_dev, jnp.int32).at[slot_index].set(pair_rows // fan_out)
+    hit = slot_index[:, None] == jnp.arange(slot_count, dtype=jnp.int32)[None, :]
+    source_row = jnp.min(jnp.where(hit, (pair_rows // fan_out)[:, None], tok_dev), axis=0)
+    slot_weight = jnp.sum(
+        jnp.where(hit, combine.reshape(-1).astype(jnp.bfloat16).astype(jnp.float32)[:, None], 0.0), axis=0
+    ).astype(jnp.bfloat16)
+    empty_tile = jnp.zeros((1, tile_rows, lanes), jnp.bfloat16)
+    weight_tiles = jnp.pad(
+        slot_weight.reshape(owners, 1, capacity), ((0, 0), (0, tile_rows - 1), (0, lanes - capacity))
     )
-    slot_weight = (
-        jnp.zeros((slot_count,), jnp.bfloat16)
-        .at[slot_index]
-        .set(combine.reshape(-1).astype(jnp.bfloat16))
-    )
-    token_table = jnp.concatenate(
+    table = jnp.concatenate(
         [
-            jnp.concatenate([x_dith, g_dith], axis=1),
-            jnp.zeros((1, 2 * model_width), jnp.bfloat16),
+            x_dith.reshape(tok_dev, tile_rows, lanes),
+            empty_tile,
+            g_dith.reshape(tok_dev, tile_rows, lanes),
+            empty_tile,
+            weight_tiles,
         ],
         axis=0,
     )
-    weight_cols = jnp.pad(slot_weight[:, None], ((0, 0), (0, lane - 1)))
-    send = jnp.concatenate([token_table[source_row], weight_cols], axis=1)
-    recv = lax.all_to_all(
-        send.reshape(owners, capacity, send.shape[1]), "expert", split_axis=0, concat_axis=0, tiled=True
-    ).reshape(slot_count, send.shape[1])
-    row_x = recv[:, :model_width]
-    row_g = recv[:, model_width : 2 * model_width]
-    weight = recv[:, 2 * model_width : 2 * model_width + 1].astype(jnp.float32)
+    rows_by_dest = source_row.reshape(owners, capacity)
+    weight_base = 2 * (tok_dev + 1)
+    tile_index = jnp.concatenate(
+        [
+            rows_by_dest,
+            rows_by_dest + (tok_dev + 1),
+            weight_base + jnp.arange(owners, dtype=jnp.int32)[:, None],
+        ],
+        axis=1,
+    )
+    wire = lax.all_to_all(table[tile_index], "expert", split_axis=0, concat_axis=0, tiled=True)
+    row_x = wire[:, :capacity].reshape(slot_count, model_width)
+    row_g = wire[:, capacity : 2 * capacity].reshape(slot_count, model_width)
+    weight = wire[:, 2 * capacity, 0, :capacity].reshape(slot_count, 1).astype(jnp.float32)
     gate_w = w_gate[0]
     up_w = w_up[0]
     down_w = w_down[0]
@@ -95,21 +106,21 @@
         jnp.dot(gate_rows_grad, gate_w.T, preferred_element_type=jnp.float32)
         + jnp.dot(up_rows_grad, up_w.T, preferred_element_type=jnp.float32)
     ).astype(jnp.bfloat16)
+    comb_tile = jnp.pad(
+        comb_slot.reshape(owners, 1, 1, capacity), ((0, 0), (0, 0), (0, tile_rows - 1), (0, lanes - capacity))
+    )
     back_send = jnp.concatenate(
-        [row_grad, jnp.pad(comb_slot[:, None], ((0, 0), (0, lane - 1)))], axis=1
+        [row_grad.reshape(owners, capacity, tile_rows, lanes), comb_tile], axis=1
     )
-    back = lax.all_to_all(
-        back_send.reshape(owners, capacity, back_send.shape[1]),
-        "expert",
-        split_axis=0,
-        concat_axis=0,
-        tiled=True,
-    ).reshape(slot_count, back_send.shape[1])
-    back_flat = back[slot_index]
-    grad_tokens = jnp.sum(
-        back_flat[:, :model_width].reshape(tok_dev, fan_out, model_width).astype(jnp.float32), axis=1
-    ).astype(jnp.bfloat16)
-    grad_combine = back_flat[:, model_width].reshape(tok_dev, fan_out)
+    back = lax.all_to_all(back_send, "expert", split_axis=0, concat_axis=0, tiled=True)
+    back_rows = back[:, :capacity].reshape(slot_count, tile_rows, lanes)
+    back_comb = back[:, capacity, 0, :capacity].reshape(slot_count)
+    grad_tokens = (
+        jnp.sum(back_rows[slot_index].reshape(tok_dev, fan_out, tile_rows, lanes).astype(jnp.float32), axis=1)
+        .astype(jnp.bfloat16)
+        .reshape(tok_dev, model_width)
+    )
+    grad_combine = back_comb[slot_index].reshape(tok_dev, fan_out)
     gate_grad = reduced[:, :hidden_units]
     up_grad = reduced[:, hidden_units : 2 * hidden_units]
     down_grad = reduced[:, 2 * hidden_units :].T

time: 271 us -> 223 us (0.82)
  local copies, waits for them, and re-layouts: 48.5 us -> 31.1 us
  blocking collectives: 110 us -> 93.1 us
  other arithmetic: 20.1 us -> 12 us
  waiting for transfers between devices: 50.7 us -> 43.8 us
  matrix products: 17.6 us -> 20.4 us
    all_to_all x1, blocking collectives: 110 us -> 93.1 us  [body(): lax.all_to_all(table[tile_index], 'expert', split_axis=0, concat_axis=0,...]
    reshape x4 -> x2, local copies, waits for them, and re-layouts: 15.9 us -> 0.18 us  [the longest x1 0.09 us: body(): grad_combine = back_comb[slot_index].reshape(tok_dev, fan_out)]
    all_to_all x1, waiting for transfers between devices: 50.7 us -> 43.8 us  [body(): lax.all_to_all(back_send, 'expert', split_axis=0, concat_axis=0, tiled=True)]
    scatter x2 -> x0, local copies, waits for them, and re-layouts: 5.86 us -> none  [the longest x1 2.95 us: body(): slot_weight = jnp.zeros((slot_count,), jnp.bfloat16).at[slot_index].set(c...]
    gather x2 -> x3, local copies, waits for them, and re-layouts: 16.4 us -> 10.6 us  [the longest x1 4.29 us: body(): table[tile_index]]
    slice x3 -> x5, local copies, waits for them, and re-layouts: 2.54 us -> 7.18 us  [the longest x1 2.98 us: body(): back_rows = back[:, :capacity].reshape(slot_count, tile_rows, lanes)]
    concatenate x3 -> x2, other arithmetic: 6.22 us -> 1.6 us  [the longest x1 1.6 us: body(): jnp.concatenate([row_grad.reshape(owners, capacity, tile_rows, lanes), co...]
    unnamed x18 -> x34, local copies, waits for them, and re-layouts: 4.75 us -> 8.97 us
where the time goes in v2:
time: 223 us; the launch traced here: 222 us
  blocking collectives  93.1 us (42%)
  waiting for transfers between devices  43.8 us (20%)
  local copies, waits for them, and re-layouts  31.1 us (14%)
  matrix products  20.4 us (9%)
  between operations  15.6 us (7%)
  other arithmetic  12 us (5%)
  starting transfers between devices  6.08 us (3%)
    all_to_all x1, blocking collectives, body(): lax.all_to_all(table[tile_index], 'expert', split_axis=0, concat_axis=0,...  93.1 us
    all_to_all x1, waiting for transfers between devices, body(): lax.all_to_all(back_send, 'expert', split_axis=0, concat_axis=0, tiled=True)  43.8 us
    unnamed x34, local copies, waits for them, and re-layouts  8.97 us
    all_to_all x1, starting transfers between devices, body(): lax.all_to_all(back_send, 'expert', split_axis=0, concat_axis=0, tiled=True)  6.04 us
    dot_general x1, matrix products, body(): back_grad = jnp.dot(row_g, down_w.T, preferred_element_type=jnp.float32)  5.39 us
    concatenate x1, other arithmetic, body(): jnp.concatenate([gate_part.astype(jnp.bfloat16), up_part.astype(jnp.bfloa...  4.48 us
  transfers between devices with their start and end apart: 2, of which 1 were waited for; matrix products, arithmetic and copies ran while one was open for 9% of the time, Pallas kernels for 0%

profile of v2, /device:TPU:8, one launch (start us, length us, event | category | flops | bytes accessed | tf_op | source)
XLA Modules:
  0.0 222.2 jit_solution(5965512150482684015)
XLA Ops:
  7.2 0.9 copy.38
  9.9 1.3 fusion.80
  12.6 2.7 %fusion.69 = (bf16[6,8,16,128]{3,1,2,0:T(8,128)(2,1)S(1)}, bf16[6,8,16,128]{3,1,2,0:T(8,128)(2,1)S(1)}) fusion(bf16[48,2048]{1,0:T(8,128)(2,1)} %param.9, s32[]{:T(128)S(6)} %xor.58, s32[48]{0:T(128)S(1)} %add_multiply_fusion, s32[]{:T(128)S(6)} %xor.50, bf16[48,2048]{1,0:T(8,128)(2,1)} %param.8), kind=kLoop, calls=%fused_computation.119 | loop fusion | flops 13074432 | bytes 786632
  19.4 4.3 %gather_fusion = bf16[864,16,128]{2,1,0:T(8,128)(2,1)} fusion(bf16[130,16,128]{2,1,0:T(8,128)(2,1)} %pad_dynamic-update-slice_fusion, s32[1024]{0:T(1024)S(1)} %pad_clamp_fusion.1), kind=kCustom, calls=%fused_computation | custom fusion | bytes 7081344 | tf_op jit(solution)/shard_map/gather | solution.py:76
  23.7 93.1 %all_to_all.10 = bf16[32,27,16,128]{3,2,1,0:T(8,128)(2,1)S(1)} all-to-all(bf16[32,27,16,128]{3,2,1,0:T(8,128)(2,1)} %bitcast.93), channel_id=1, replica_groups=mesh['dp'=8,'expert'=32] {'expert'}, dimensions={0} | all-to-all | bytes 7077888 | tf_op jit(solution)/shard_map/all_to_all | solution.py:76
  116.8 1.8 fusion.79
  119.3 2.5 %fusion.7 = f32[416,768]{1,0:T(8,128)} fusion(bf16[1,2048,768]{2,1,0:T(8,128)(2,1)S(1)} %copy-done.6, bf16[52,8,16,128]{3,2,1,0:T(8,128)(2,1)S(1)} %bitcast.97), kind=kOutput, calls=%fused_computation.17 | convolution fusion | flops 1308622848 | bytes 6127616 | tf_op jit(solution)/shard_map/dot_general | solution.py:84
  121.9 2.6 %fusion.3 = f32[416,768]{1,0:T(8,128)} fusion(bf16[1,2048,768]{2,1,0:T(8,128)(2,1)S(1)} %copy-done, bf16[52,8,16,128]{3,2,1,0:T(8,128)(2,1)S(1)} %bitcast.98), kind=kOutput, calls=%fused_computation.13 | convolution fusion | flops 1308622848 | bytes 6127616 | tf_op jit(solution)/shard_map/dot_general | solution.py:83
  124.6 5.4 %multiply_reduce_fusion = (bf16[416]{0:T(512)(128)(2,1)S(1)}, bf16[416,768]{1,0:T(8,128)(2,1)S(1)}, bf16[416,768]{1,0:T(8,128)(2,1)S(1)}, bf16[416,768]{1,0:T(8,128)(2,1)S(1)}) fusion(f32[416,768]{1,0:T(8,128)} %fusion.7, f32[416,768]{1,0:T(8,128)} %fusion.3, f32[416]{0:T(512)S(1)} %reshape.282, bf16[1,768,2048]{2,1,0:T(8,128)(2,1)} %param.14, ...), kind=kOutput, calls=%fused_computation.32 | convolution fusion | flops 1314692736 | bytes 9324992 | tf_op jit(solution)/shard_map/dot_general | solution.py:88
  130.0 2.0 convolution_convert_fusion
  132.0 1.9 convolution_convert_fusion.1
  133.9 1.9 convolution_convert_fusion.2
  135.7 4.5 %pad_maximum_fusion = bf16[2048,2304]{0,1:T(8,128)(2,1)} fusion(bf16[2048,768]{0,1:T(8,128)(2,1)S(1)} %convolution_convert_fusion, bf16[2048,768]{0,1:T(8,128)(2,1)S(1)} %convolution_convert_fusion.1, bf16[2048,768]{0,1:T(8,128)(2,1)S(1)} %convolution_convert_fusion.2), kind=kLoop, calls=%fused_computation.3 | loop fusion | flops 28311552 | bytes 18874368 | tf_op jit(solution)/shard_map/concatenate | solution.py:100
  140.4 2.7 %fusion.1 = f32[416,2048]{1,0:T(8,128)S(1)} fusion(bf16[416,768]{1,0:T(8,128)(2,1)} %copy-done.8, bf16[1,2048,768]{2,1,0:T(8,128)(2,1)S(1)} %copy-done), kind=kOutput, calls=%fused_computation.11 | convolution fusion | flops 1308622848 | bytes 7192576 | tf_op jit(solution)/shard_map/dot_general | solution.py:106
  143.2 1.5 fusion.21
  145.1 1.6 fusion.13
  146.7 6.0 %all-to-all-start.1 = ((bf16[32,14,16,128]{3,2,1,0:T(8,128)(2,1)}), bf16[32,14,16,128]{3,2,1,0:T(8,128)(2,1)}, u32[]{:S(2)}, u32[]{:S(2)}) async-start(bf16[32,14,16,128]{3,2,1,0:T(8,128)(2,1)} %fusion.13), calls=%async_computation.1 | async-start | bytes 3670016 | tf_op jit(solution)/shard_map/all_to_all | solution.py:115
  153.0 43.8 %all-to-all-done.1 = bf16[32,14,16,128]{3,2,1,0:T(8,128)(2,1)} async-done(((bf16[32,14,16,128]{3,2,1,0:T(8,128)(2,1)}), bf16[32,14,16,128]{3,2,1,0:T(8,128)(2,1)}, u32[]{:S(2)}, u32[]{:S(2)}) %all-to-all-start.1) | async-done | bytes 1835040 | tf_op jit(solution)/shard_map/all_to_all | solution.py:115
  196.8 3.0 %slice.58 = bf16[32,13,16,128]{3,2,1,0:T(8,128)(2,1)} slice(bf16[32,14,16,128]{3,2,1,0:T(8,128)(2,1)} %all-to-all-done.1), slice={[0:32], [0:13], [0:16], [0:128]} | slice | bytes 3407872 | tf_op jit(solution)/shard_map/slice | solution.py:116
  199.8 3.5 %gather_fusion.1 = bf16[384,16,128]{2,1,0:T(8,128)(2,1)} fusion(bf16[416,16,128]{2,1,0:T(8,128)(2,1)} %bitcast.95, s32[1024]{0:T(1024)S(1)} %pad_clamp_fusion), kind=kCustom, calls=%fused_computation.1 | custom fusion | bytes 3147264 | tf_op jit(solution)/shard_map/gather | solution.py:119
  203.3 1.7 reduce_sum.45
  206.8 2.8 %gather_fusion.2 = bf16[384]{0:T(512)(128)(2,1)S(1)} fusion(bf16[416]{0:T(512)(128)(2,1)S(1)} %reshape_squeeze.4, s32[1024]{0:T(1024)S(1)} %pad_clamp_fusion), kind=kCustom, calls=%fused_computation.2 | custom fusion | bytes 3072 | tf_op jit(solution)/shard_map/gather | solution.py:123
  210.3 2.2 slice_bitcast_fusion
  212.5 1.9 copy.47
  (70 shorter events, 11.0 us)
Async XLA Ops:
  7.2 114.7 %copy-start = (bf16[1,2048,768]{2,1,0:T(8,128)(2,1)S(1)}, bf16[1,2048,768]{2,1,0:T(8,128)(2,1)}, u32[]{:S(2)}) copy-start(bf16[1,2048,768]{2,1,0:T(8,128)(2,1)} %param.12) | copy-start | bytes 9437188
  7.2 10.7 %copy-start.5 = (f32[48,8]{0,1:T(8,128)S(1)}, f32[48,8]{0,1:T(8,128)}, u32[]{:S(2)}) copy-start(f32[48,8]{0,1:T(8,128)} %param.11) | copy-start | bytes 4612
  7.2 203.1 %reduce-scatter.2.cloned.1.call-start = ((), (), s32[]{:S(2)}) async-start(), calls=%async_computation.3 | async-start | bytes 10616832 | tf_op jit(solution)/shard_map/reduce_scatter | solution.py:104
  116.8 2.5 %copy-start.6 = (bf16[1,2048,768]{2,1,0:T(8,128)(2,1)S(1)}, bf16[1,2048,768]{2,1,0:T(8,128)(2,1)}, u32[]{:S(2)}) copy-start(bf16[1,2048,768]{2,1,0:T(8,128)(2,1)} %param.13) | copy-start | bytes 9437188
  118.6 3.3 %copy-start.1 = (bf16[32,13,16,128]{3,2,1,0:T(8,128)(2,1)}, bf16[32,13,16,128]{3,2,1,0:T(8,128)(2,1)S(1)}, u32[]{:S(2)}) copy-start(bf16[32,13,16,128]{3,2,1,0:T(8,128)(2,1)S(1)} %get-tuple-element.28) | copy-start | bytes 5111812
  124.6 5.4 %copy-start.3 = (bf16[32,13,16,128]{3,2,1,0:T(8,128)(2,1)S(1)}, bf16[32,13,16,128]{3,2,1,0:T(8,128)(2,1)}, u32[]{:S(2)}) copy-start(bf16[32,13,16,128]{3,2,1,0:T(8,128)(2,1)} %get-tuple-element.29) | copy-start | bytes 5111812
  130.0 2.0 copy-start.9
  130.0 3.9 %copy-start.8 = (bf16[416,768]{1,0:T(8,128)(2,1)}, bf16[416,768]{1,0:T(8,128)(2,1)S(1)}, u32[]{:S(2)}) copy-start(bf16[416,768]{1,0:T(8,128)(2,1)S(1)} %get-tuple-element.27) | copy-start | bytes 1916932
  130.0 2.0 copy-start.2
  140.4 2.8 %copy-start.7 = (bf16[1,2048,768]{2,1,0:T(8,128)(2,1)S(1)}, bf16[1,2048,768]{2,1,0:T(8,128)(2,1)}, u32[]{:S(2)}) copy-start(bf16[1,2048,768]{2,1,0:T(8,128)(2,1)} %param.13) | copy-start | bytes 9437188
  140.4 2.8 %copy-start.10 = (bf16[416,768]{1,0:T(8,128)(2,1)S(1)}, bf16[416,768]{1,0:T(8,128)(2,1)}, u32[]{:S(2)}) copy-start(bf16[416,768]{1,0:T(8,128)(2,1)} %copy-done.9) | copy-start | bytes 1916932
  146.7 6.1 %copy-start.4 = (s32[48,8]{0,1:T(8,128)S(1)}, s32[48,8]{0,1:T(8,128)}, u32[]{:S(2)}) copy-start(s32[48,8]{0,1:T(8,128)} %param.10) | copy-start | bytes 4612
  146.7 50.1 %all-to-all-start.1 = ((bf16[32,14,16,128]{3,2,1,0:T(8,128)(2,1)}), bf16[32,14,16,128]{3,2,1,0:T(8,128)(2,1)}, u32[]{:S(2)}, u32[]{:S(2)}) async-start(bf16[32,14,16,128]{3,2,1,0:T(8,128)(2,1)} %fusion.13), calls=%async_computation.1 | async-start | bytes 3670016 | tf_op jit(solution)/shard_map/all_to_all | solution.py:115
Sparse Core Ops, SparseCore 0:
  140.4 56.6 reduce-scatter.1

commit v3 on v2

--- a/solution.py
+++ b/solution.py
@@ -50,77 +50,96 @@
         jnp.where(hit, combine.reshape(-1).astype(jnp.bfloat16).astype(jnp.float32)[:, None], 0.0), axis=0
     ).astype(jnp.bfloat16)
     empty_tile = jnp.zeros((1, tile_rows, lanes), jnp.bfloat16)
-    weight_tiles = jnp.pad(
-        slot_weight.reshape(owners, 1, capacity), ((0, 0), (0, tile_rows - 1), (0, lanes - capacity))
-    )
     table = jnp.concatenate(
         [
             x_dith.reshape(tok_dev, tile_rows, lanes),
             empty_tile,
             g_dith.reshape(tok_dev, tile_rows, lanes),
             empty_tile,
-            weight_tiles,
         ],
         axis=0,
     )
     rows_by_dest = source_row.reshape(owners, capacity)
-    weight_base = 2 * (tok_dev + 1)
-    tile_index = jnp.concatenate(
-        [
-            rows_by_dest,
-            rows_by_dest + (tok_dev + 1),
-            weight_base + jnp.arange(owners, dtype=jnp.int32)[:, None],
-        ],
-        axis=1,
-    )
-    wire = lax.all_to_all(table[tile_index], "expert", split_axis=0, concat_axis=0, tiled=True)
-    row_x = wire[:, :capacity].reshape(slot_count, model_width)
-    row_g = wire[:, capacity : 2 * capacity].reshape(slot_count, model_width)
-    weight = wire[:, 2 * capacity, 0, :capacity].reshape(slot_count, 1).astype(jnp.float32)
+    weight_by_dest = slot_weight.reshape(owners, capacity)
     gate_w = w_gate[0]
     up_w = w_up[0]
     down_w = w_down[0]
-    gate_pre = jnp.dot(row_x, gate_w, preferred_element_type=jnp.float32)
-    up_pre = jnp.dot(row_x, up_w, preferred_element_type=jnp.float32)
-    sigmoid_val = jax.nn.sigmoid(gate_pre)
-    silu_val = gate_pre * sigmoid_val
-    hidden = (silu_val * up_pre).astype(jnp.bfloat16)
-    back_grad = jnp.dot(row_g, down_w.T, preferred_element_type=jnp.float32)
-    comb_slot = jnp.sum(hidden.astype(jnp.float32) * back_grad, axis=1).astype(jnp.bfloat16)
-    hidden_grad = weight * back_grad
-    gate_rows_grad = (
-        hidden_grad * up_pre * sigmoid_val * (1.0 + gate_pre * (1.0 - sigmoid_val))
-    ).astype(jnp.bfloat16)
-    up_rows_grad = (hidden_grad * silu_val).astype(jnp.bfloat16)
-    scaled_grad = (weight * row_g.astype(jnp.float32)).astype(jnp.bfloat16)
-    gate_part = jnp.dot(row_x.T, gate_rows_grad, preferred_element_type=jnp.float32)
-    up_part = jnp.dot(row_x.T, up_rows_grad, preferred_element_type=jnp.float32)
-    down_part_t = jnp.dot(scaled_grad.T, hidden, preferred_element_type=jnp.float32)
     hidden_units = gate_w.shape[1]
+    first = (capacity + 1) // 2
+    chunks = ((0, first), (first, capacity - first))
+    gate_acc = up_acc = down_acc = None
+    back_tables = []
+    back_combs = []
+    sends = []
+    for lo, size in chunks:
+        rows = rows_by_dest[:, lo : lo + size]
+        weight_tile = jnp.pad(
+            weight_by_dest[:, None, lo : lo + size], ((0, 0), (0, tile_rows - 1), (0, lanes - size))
+        )
+        sends.append(
+            jnp.concatenate([table[rows], table[rows + (tok_dev + 1)], weight_tile[:, None]], axis=1)
+        )
+    wire = None
+    for (lo, size), send in zip(chunks, sends):
+        if wire is not None:
+            wire, send = lax.optimization_barrier((wire, send))
+        wire = lax.all_to_all(send, "expert", split_axis=0, concat_axis=0, tiled=True)
+        count = owners * size
+        row_x = wire[:, :size].reshape(count, model_width)
+        row_g = wire[:, size : 2 * size].reshape(count, model_width)
+        weight = wire[:, 2 * size, 0, :size].reshape(count, 1).astype(jnp.float32)
+        gate_pre = jnp.dot(row_x, gate_w, preferred_element_type=jnp.float32)
+        up_pre = jnp.dot(row_x, up_w, preferred_element_type=jnp.float32)
+        sigmoid_val = jax.nn.sigmoid(gate_pre)
+        silu_val = gate_pre * sigmoid_val
+        hidden = (silu_val * up_pre).astype(jnp.bfloat16)
+        back_grad = jnp.dot(row_g, down_w.T, preferred_element_type=jnp.float32)
+        comb_slot = jnp.sum(hidden.astype(jnp.float32) * back_grad, axis=1).astype(jnp.bfloat16)
+        hidden_grad = weight * back_grad
+        gate_rows_grad = (
+            hidden_grad * up_pre * sigmoid_val * (1.0 + gate_pre * (1.0 - sigmoid_val))
+        ).astype(jnp.bfloat16)
+        up_rows_grad = (hidden_grad * silu_val).astype(jnp.bfloat16)
+        scaled_grad = (weight * row_g.astype(jnp.float32)).astype(jnp.bfloat16)
+        gate_part = jnp.dot(row_x.T, gate_rows_grad, preferred_element_type=jnp.float32)
+        up_part = jnp.dot(row_x.T, up_rows_grad, preferred_element_type=jnp.float32)
+        down_part_t = jnp.dot(scaled_grad.T, hidden, preferred_element_type=jnp.float32)
+        if gate_acc is None:
+            gate_acc, up_acc, down_acc = gate_part, up_part, down_part_t
+        else:
+            gate_acc, up_acc, down_acc = gate_acc + gate_part, up_acc + up_part, down_acc + down_part_t
+        row_grad = (
+            jnp.dot(gate_rows_grad, gate_w.T, preferred_element_type=jnp.float32)
+            + jnp.dot(up_rows_grad, up_w.T, preferred_element_type=jnp.float32)
+        ).astype(jnp.bfloat16)
+        comb_tile = jnp.pad(
+            comb_slot.reshape(owners, 1, 1, size), ((0, 0), (0, 0), (0, tile_rows - 1), (0, lanes - size))
+        )
+        back_send = jnp.concatenate([row_grad.reshape(owners, size, tile_rows, lanes), comb_tile], axis=1)
+        back = lax.all_to_all(back_send, "expert", split_axis=0, concat_axis=0, tiled=True)
+        back_tables.append(back.reshape(owners * (size + 1), tile_rows, lanes))
+        back_combs.append(back[:, size, 0, :size])
     parts = jnp.concatenate(
-        [gate_part.astype(jnp.bfloat16), up_part.astype(jnp.bfloat16), down_part_t.astype(jnp.bfloat16)],
+        [gate_acc.astype(jnp.bfloat16), up_acc.astype(jnp.bfloat16), down_acc.astype(jnp.bfloat16)],
         axis=1,
     )
     reduced = lax.psum_scatter(parts, "dp", scatter_dimension=0, tiled=True)
-    row_grad = (
-        jnp.dot(gate_rows_grad, gate_w.T, preferred_element_type=jnp.float32)
-        + jnp.dot(up_rows_grad, up_w.T, preferred_element_type=jnp.float32)
-    ).astype(jnp.bfloat16)
-    comb_tile = jnp.pad(
-        comb_slot.reshape(owners, 1, 1, capacity), ((0, 0), (0, 0), (0, tile_rows - 1), (0, lanes - capacity))
+    dest = slot_index // capacity
+    pos = slot_index % capacity
+    second = chunks[1][1]
+    back_index = jnp.where(
+        pos < first, dest * (first + 1) + pos, owners * (first + 1) + dest * (second + 1) + pos - first
     )
-    back_send = jnp.concatenate(
-        [row_grad.reshape(owners, capacity, tile_rows, lanes), comb_tile], axis=1
-    )
-    back = lax.all_to_all(back_send, "expert", split_axis=0, concat_axis=0, tiled=True)
-    back_rows = back[:, :capacity].reshape(slot_count, tile_rows, lanes)
-    back_comb = back[:, capacity, 0, :capacity].reshape(slot_count)
+    back_rows = jnp.concatenate(back_tables, axis=0)[back_index]
     grad_tokens = (
-        jnp.sum(back_rows[slot_index].reshape(tok_dev, fan_out, tile_rows, lanes).astype(jnp.float32), axis=1)
+        jnp.sum(back_rows.reshape(tok_dev, fan_out, tile_rows, lanes).astype(jnp.float32), axis=1)
         .astype(jnp.bfloat16)
         .reshape(tok_dev, model_width)
     )
-    grad_combine = back_comb[slot_index].reshape(tok_dev, fan_out)
+    back_comb = jnp.concatenate(back_combs, axis=1).reshape(slot_count).astype(jnp.float32)
+    grad_combine = (
+        jnp.sum(jnp.where(hit, back_comb[None, :], 0.0), axis=1).astype(jnp.bfloat16).reshape(tok_dev, fan_out)
+    )
     gate_grad = reduced[:, :hidden_units]
     up_grad = reduced[:, hidden_units : 2 * hidden_units]
     down_grad = reduced[:, 2 * hidden_units :].T

time: 223 us -> 247 us (1.11)
  blocking collectives: 93.1 us -> 0 us
  waiting for transfers between devices: 43.8 us -> 100 us
  starting transfers between devices: 6.08 us -> 30.2 us
  matrix products: 20.4 us -> 37.7 us
  other arithmetic: 12 us -> 26.2 us
  local copies, waits for them, and re-layouts: 31.1 us -> 35 us
    all_to_all x1 -> x0, blocking collectives: 93.1 us -> none  [body(): lax.all_to_all(table[tile_index], 'expert', split_axis=0, concat_axis=0,...]
    all_to_all x0 -> x2, waiting for transfers between devices: none -> 56.3 us  [body(): lax.all_to_all(send, 'expert', split_axis=0, concat_axis=0, tiled=True)]
    all_to_all x0 -> x2, starting transfers between devices: none -> 18.6 us  [body(): lax.all_to_all(send, 'expert', split_axis=0, concat_axis=0, tiled=True)]
    concatenate x3 -> x7, other arithmetic: 6.08 us -> 15.7 us  [the longest x2 5.86 us: body(): jnp.concatenate([table[rows], table[rows + (tok_dev + 1)], weight_tile[:,...]
    dot_general x1 -> x2, matrix products: 1.95 us -> 7.81 us  [body(): jnp.dot(scaled_grad.T, hidden, preferred_element_type=jnp.float32)]
    dot_general x1 -> x2, matrix products: 1.85 us -> 7.64 us  [body(): up_part = jnp.dot(row_x.T, up_rows_grad, preferred_element_type=jnp.float32)]
    all_to_all x1 -> x2, starting transfers between devices: 6.04 us -> 11.4 us  [body(): lax.all_to_all(back_send, 'expert', split_axis=0, concat_axis=0, tiled=True)]
    broadcast_in_dim x0 -> x11, local copies, waits for them, and re-layouts: none -> 4.56 us  [the longest x2 1.49 us: body(): table[rows + (tok_dev + 1)]]
  transfers between devices with their start and end apart: 2 -> 5, of which waited for: 1 -> 4; matrix products, arithmetic and copies ran while one was open for 9% -> 21% of each run, Pallas kernels for 0% -> 0%
where the time goes in v3:
time: 247 us; the launch traced here: 245 us
  waiting for transfers between devices  100 us (40%)
  matrix products  37.7 us (15%)
  local copies, waits for them, and re-layouts  35 us (14%)
  starting transfers between devices  30.2 us (12%)
  other arithmetic  26.2 us (11%)
  between operations  15.9 us (6%)
    all_to_all x2, waiting for transfers between devices, body(): lax.all_to_all(send, 'expert', split_axis=0, concat_axis=0, tiled=True)  56.3 us
    all_to_all x2, waiting for transfers between devices, body(): lax.all_to_all(back_send, 'expert', split_axis=0, concat_axis=0, tiled=True)  43.8 us
    all_to_all x2, starting transfers between devices, body(): lax.all_to_all(send, 'expert', split_axis=0, concat_axis=0, tiled=True)  18.6 us
    all_to_all x2, starting transfers between devices, body(): lax.all_to_all(back_send, 'expert', split_axis=0, concat_axis=0, tiled=True)  11.4 us
    unnamed x55, local copies, waits for them, and re-layouts  8.61 us
    dot_general x2, matrix products, body(): jnp.dot(scaled_grad.T, hidden, preferred_element_type=jnp.float32)  7.81 us
    dot_general x2, matrix products, body(): up_part = jnp.dot(row_x.T, up_rows_grad, preferred_element_type=jnp.float32)  7.64 us
    concatenate x2, other arithmetic, body(): jnp.concatenate([table[rows], table[rows + (tok_dev + 1)], weight_tile[:,...  5.86 us
  transfers between devices with their start and end apart: 5, of which 4 were waited for; matrix products, arithmetic and copies ran while one was open for 21% of the time, Pallas kernels for 0%

profile of v3, /device:TPU:8, one launch (start us, length us, event | category | flops | bytes accessed | tf_op | source)
XLA Modules:
  0.0 245.1 jit_solution(1456655498604965096)
XLA Ops:
  15.6 2.7 %fusion.112 = (bf16[6,8,16,128]{3,1,2,0:T(8,128)(2,1)S(1)}, bf16[6,8,16,128]{3,1,2,0:T(8,128)(2,1)S(1)}) fusion(bf16[48,2048]{1,0:T(8,128)(2,1)} %param.8, s32[]{:T(128)S(6)} %xor.50, s32[48]{0:T(128)S(1)} %add_multiply_fusion, s32[]{:T(128)S(6)} %xor.58, bf16[48,2048]{1,0:T(8,128)(2,1)} %param.9), kind=kLoop, calls=%fused_computation.167 | loop fusion | flops 13074432 | bytes 786632
  21.9 3.1 %pad_maximum_fusion.1 = bf16[32,15,16,128]{3,2,1,0:T(8,128)(2,1)} fusion(bf16[32,1,16,128]{3,2,1,0:T(8,128)(2,1)} %pad_bitcast_fusion.1, bf16[32,7,16,128]{3,2,1,0:T(8,128)(2,1)} %bitcast.168, bf16[32,7,16,128]{3,2,1,0:T(8,128)(2,1)} %bitcast.169), kind=kLoop, calls=%fused_computation.35 | loop fusion | flops 1966080 | bytes 3932160 | tf_op jit(solution)/shard_map/concatenate | solution.py:80
  24.9 11.7 %all-to-all-start = ((bf16[32,15,16,128]{3,2,1,0:T(8,128)(2,1)}), bf16[32,15,16,128]{3,2,1,0:T(8,128)(2,1)}, u32[]{:S(2)}, u32[]{:S(2)}) async-start(bf16[32,15,16,128]{3,2,1,0:T(8,128)(2,1)} %pad_maximum_fusion.1), calls=%async_computation | async-start | bytes 3932160 | tf_op jit(solution)/shard_map/all_to_all | solution.py:86
  45.7 2.8 %pad_maximum_fusion.3 = bf16[32,13,16,128]{3,2,1,0:T(8,128)(2,1)} fusion(bf16[32,1,16,128]{3,2,1,0:T(8,128)(2,1)S(1)} %pad_bitcast_fusion, bf16[32,6,16,128]{3,2,1,0:T(8,128)(2,1)} %bitcast.171, bf16[32,6,16,128]{3,2,1,0:T(8,128)(2,1)} %bitcast.172), kind=kLoop, calls=%fused_computation.40 | loop fusion | flops 1703936 | bytes 3407872 | tf_op jit(solution)/shard_map/concatenate | solution.py:80
  48.5 34.7 %all-to-all-done = bf16[32,15,16,128]{3,2,1,0:T(8,128)(2,1)} async-done(((bf16[32,15,16,128]{3,2,1,0:T(8,128)(2,1)}), bf16[32,15,16,128]{3,2,1,0:T(8,128)(2,1)}, u32[]{:S(2)}, u32[]{:S(2)}) %all-to-all-start) | async-done | bytes 1966112 | tf_op jit(solution)/shard_map/all_to_all | solution.py:86
  83.3 6.8 %all-to-all-start.2 = ((bf16[32,13,16,128]{3,2,1,0:T(8,128)(2,1)}), bf16[32,13,16,128]{3,2,1,0:T(8,128)(2,1)}, u32[]{:S(2)}, u32[]{:S(2)}) async-start(bf16[32,13,16,128]{3,2,1,0:T(8,128)(2,1)} %pad_maximum_fusion.3), calls=%async_computation.2 | async-start | bytes 3407872 | tf_op jit(solution)/shard_map/all_to_all | solution.py:86
  98.4 3.7 %fusion.43 = f32[2048,768]{0,1:T(8,128)} fusion(bf16[224,768]{1,0:T(8,128)(2,1)S(1)} %get-tuple-element.42, bf16[28,8,16,128]{3,2,1,0:T(8,128)(2,1)S(1)} %bitcast.162), kind=kOutput, calls=%fused_computation.47 | convolution fusion | flops 704643072 | bytes 7553024 | tf_op jit(solution)/shard_map/dot_general | solution.py:105
  102.1 3.7 %fusion.45 = f32[2048,768]{0,1:T(8,128)} fusion(bf16[224,768]{1,0:T(8,128)(2,1)S(1)} %get-tuple-element.36, bf16[28,8,16,128]{3,2,1,0:T(8,128)(2,1)S(1)} %bitcast.163), kind=kOutput, calls=%fused_computation.49 | convolution fusion | flops 704643072 | bytes 7553024 | tf_op jit(solution)/shard_map/dot_general | solution.py:104
  105.8 3.7 %fusion.42 = f32[2048,768]{0,1:T(8,128)} fusion(bf16[224,768]{1,0:T(8,128)(2,1)S(1)} %get-tuple-element.33, f32[224]{0:T(256)S(1)} %reshape.269, bf16[28,8,16,128]{3,2,1,0:T(8,128)(2,1)S(1)} %bitcast.166), kind=kOutput, calls=%fused_computation.46 | convolution fusion | flops 706019328 | bytes 7553920 | tf_op jit(solution)/shard_map/dot_general | solution.py:106
  109.5 21.6 %all-to-all-done.2 = bf16[32,13,16,128]{3,2,1,0:T(8,128)(2,1)} async-done(((bf16[32,13,16,128]{3,2,1,0:T(8,128)(2,1)}), bf16[32,13,16,128]{3,2,1,0:T(8,128)(2,1)}, u32[]{:S(2)}, u32[]{:S(2)}) %all-to-all-start.2) | async-done | bytes 1703968 | tf_op jit(solution)/shard_map/all_to_all | solution.py:86
  131.1 2.7 %fusion.123 = (bf16[32,6,16,128]{3,2,1,0:T(8,128)(2,1)S(1)}, bf16[32,6,16,128]{3,2,1,0:T(8,128)(2,1)}) fusion(bf16[32,13,16,128]{3,2,1,0:T(8,128)(2,1)} %all-to-all-done.2), kind=kLoop, calls=%fused_computation.212 | loop fusion | bytes 3145728 | tf_op jit(solution)/shard_map/slice | solution.py:88
  138.0 4.0 %multiply_reduce_fusion.1 = (bf16[192]{0:T(256)(128)(2,1)S(1)}, bf16[192,768]{1,0:T(8,128)(2,1)S(1)}, bf16[192,768]{1,0:T(8,128)(2,1)S(1)}, bf16[192,768]{1,0:T(8,128)(2,1)S(1)}) fusion(f32[192,768]{1,0:T(8,128)} %fusion.10, f32[192,768]{1,0:T(8,128)} %fusion.2, f32[192]{0:T(256)S(1)} %reshape.270, bf16[1,768,2048]{2,1,0:T(8,128)(2,1)} %param.14, ...), kind=kOutput, calls=%fused_computation.109 | convolution fusion | flops 606781248 | bytes 5997696 | tf_op jit(solution)/shard_map/dot_general | solution.py:96
  142.1 4.1 %add_convert_fusion = bf16[2048,768]{0,1:T(8,128)(2,1)S(1)} fusion(f32[2048,768]{0,1:T(8,128)} %fusion.42, bf16[192,768]{1,0:T(8,128)(2,1)S(1)} %get-tuple-element.35, f32[192]{0:T(256)S(1)} %reshape.270, bf16[24,8,16,128]{3,2,1,0:T(8,128)(2,1)S(1)} %bitcast.174), kind=kOutput, calls=%fused_computation.6 | convolution fusion | flops 608305152 | bytes 10519296 | tf_op jit(solution)/shard_map/dot_general | solution.py:106
  146.2 4.0 %add_convert_fusion.1 = bf16[2048,768]{0,1:T(8,128)(2,1)S(1)} fusion(f32[2048,768]{0,1:T(8,128)} %fusion.43, bf16[192,768]{1,0:T(8,128)(2,1)S(1)} %get-tuple-element.46, bf16[24,8,16,128]{3,2,1,0:T(8,128)(2,1)S(1)} %bitcast.158), kind=kOutput, calls=%fused_computation.7 | convolution fusion | flops 607125504 | bytes 10518528 | tf_op jit(solution)/shard_map/dot_general | solution.py:105
  151.5 4.5 %pad_maximum_fusion = bf16[2048,2304]{0,1:T(8,128)(2,1)} fusion(bf16[2048,768]{0,1:T(8,128)(2,1)S(1)} %add_convert_fusion, bf16[2048,768]{0,1:T(8,128)(2,1)S(1)} %add_convert_fusion.1, bf16[2048,768]{0,1:T(8,128)(2,1)S(1)} %add_convert_fusion.2), kind=kLoop, calls=%fused_computation.5 | loop fusion | flops 28311552 | bytes 18874368 | tf_op jit(solution)/shard_map/concatenate | solution.py:122
  156.1 2.2 fusion.4
  160.9 5.7 %all-to-all-start.1 = ((bf16[32,8,16,128]{3,2,1,0:T(8,128)(2,1)}), bf16[32,8,16,128]{3,2,1,0:T(8,128)(2,1)}, u32[]{:S(2)}, u32[]{:S(2)}) async-start(bf16[32,8,16,128]{3,2,1,0:T(8,128)(2,1)} %fusion.40), calls=%async_computation.1 | async-start | bytes 2097152 | tf_op jit(solution)/shard_map/all_to_all | solution.py:119
  166.8 2.3 fusion
  171.6 21.5 %all-to-all-done.1 = bf16[32,8,16,128]{3,2,1,0:T(8,128)(2,1)} async-done(((bf16[32,8,16,128]{3,2,1,0:T(8,128)(2,1)}), bf16[32,8,16,128]{3,2,1,0:T(8,128)(2,1)}, u32[]{:S(2)}, u32[]{:S(2)}) %all-to-all-start.1) | async-done | bytes 1048608 | tf_op jit(solution)/shard_map/all_to_all | solution.py:119
  193.1 5.6 %all-to-all-start.3 = ((bf16[32,7,16,128]{3,2,1,0:T(8,128)(2,1)}), bf16[32,7,16,128]{3,2,1,0:T(8,128)(2,1)}, u32[]{:S(2)}, u32[]{:S(2)}) async-start(bf16[32,7,16,128]{3,2,1,0:T(8,128)(2,1)} %fusion.41), calls=%async_computation.3 | async-start | bytes 1835008 | tf_op jit(solution)/shard_map/all_to_all | solution.py:119
  199.9 22.3 %all-to-all-done.3 = bf16[32,7,16,128]{3,2,1,0:T(8,128)(2,1)} async-done(((bf16[32,7,16,128]{3,2,1,0:T(8,128)(2,1)}), bf16[32,7,16,128]{3,2,1,0:T(8,128)(2,1)}, u32[]{:S(2)}, u32[]{:S(2)}) %all-to-all-start.3) | async-done | bytes 917536 | tf_op jit(solution)/shard_map/all_to_all | solution.py:119
  224.3 2.9 %pad_maximum_fusion.2 = bf16[480,16,128]{2,1,0:T(8,128)(2,1)} fusion(bf16[224,16,128]{2,1,0:T(8,128)(2,1)} %bitcast.15, bf16[256,16,128]{2,1,0:T(8,128)(2,1)} %bitcast.10), kind=kLoop, calls=%fused_computation.36 | loop fusion | flops 983040 | bytes 3932160 | tf_op jit(solution)/shard_map/concatenate | solution.py:133
  227.2 3.6 %gather_fusion.4 = bf16[384,16,128]{2,1,0:T(8,128)(2,1)} fusion(bf16[480,16,128]{2,1,0:T(8,128)(2,1)} %pad_maximum_fusion.2, s32[1024]{0:T(1024)S(1)} %pad_clamp_fusion), kind=kCustom, calls=%fused_computation.4 | custom fusion | bytes 3147264 | tf_op jit(solution)/shard_map/gather | solution.py:133
  233.3 2.2 slice_bitcast_fusion
  (130 shorter events, 47.1 us)
Async XLA Ops:
  7.2 86.0 %copy-start = (bf16[1,2048,768]{2,1,0:T(8,128)(2,1)S(1)}, bf16[1,2048,768]{2,1,0:T(8,128)(2,1)}, u32[]{:S(2)}) copy-start(bf16[1,2048,768]{2,1,0:T(8,128)(2,1)} %param.12) | copy-start | bytes 9437188
  14.6 3.7 %copy-start.12 = (s32[32,13]{1,0:T(8,128)}, s32[32,13]{1,0:T(8,128)S(1)}, u32[]{:S(2)}) copy-start(s32[32,13]{1,0:T(8,128)S(1)} %reshape.257) | copy-start | bytes 4996
  21.9 14.8 %copy-start.14 = (bf16[32,13]{1,0:T(8,128)(2,1)S(1)}, bf16[32,13]{1,0:T(8,128)(2,1)}, u32[]{:S(2)}) copy-start(bf16[32,13]{1,0:T(8,128)(2,1)} %copy-done.13) | copy-start | bytes 2500
  24.9 58.3 %all-to-all-start = ((bf16[32,15,16,128]{3,2,1,0:T(8,128)(2,1)}), bf16[32,15,16,128]{3,2,1,0:T(8,128)(2,1)}, u32[]{:S(2)}, u32[]{:S(2)}) async-start(bf16[32,15,16,128]{3,2,1,0:T(8,128)(2,1)} %pad_maximum_fusion.1), calls=%async_computation | async-start | bytes 3932160 | tf_op jit(solution)/shard_map/all_to_all | solution.py:86
  83.3 47.8 %all-to-all-start.2 = ((bf16[32,13,16,128]{3,2,1,0:T(8,128)(2,1)}), bf16[32,13,16,128]{3,2,1,0:T(8,128)(2,1)}, u32[]{:S(2)}, u32[]{:S(2)}) async-start(bf16[32,13,16,128]{3,2,1,0:T(8,128)(2,1)} %pad_maximum_fusion.3), calls=%async_computation.2 | async-start | bytes 3407872 | tf_op jit(solution)/shard_map/all_to_all | solution.py:86
  90.1 143.2 %reduce-scatter.2.cloned.1.call-start = ((), (), s32[]{:S(2)}) async-start(), calls=%async_computation.5 | async-start | bytes 10616832 | tf_op jit(solution)/shard_map/reduce_scatter | solution.py:126
  93.1 1.9 copy-start.1
  98.4 3.7 %copy-start.8 = (bf16[224,768]{1,0:T(8,128)(2,1)}, bf16[224,768]{1,0:T(8,128)(2,1)S(1)}, u32[]{:S(2)}) copy-start(bf16[224,768]{1,0:T(8,128)(2,1)S(1)} %get-tuple-element.36) | copy-start | bytes 1032196
  131.1 4.3 %copy-start.2 = (bf16[1,2048,768]{2,1,0:T(8,128)(2,1)S(1)}, bf16[1,2048,768]{2,1,0:T(8,128)(2,1)}, u32[]{:S(2)}) copy-start(bf16[1,2048,768]{2,1,0:T(8,128)(2,1)} %param.13) | copy-start | bytes 9437188
  133.7 3.3 %copy-start.5 = (bf16[32,6,16,128]{3,2,1,0:T(8,128)(2,1)}, bf16[32,6,16,128]{3,2,1,0:T(8,128)(2,1)S(1)}, u32[]{:S(2)}) copy-start(bf16[32,6,16,128]{3,2,1,0:T(8,128)(2,1)S(1)} %get-tuple-element.40) | copy-start | bytes 2359300
  138.0 4.0 %copy-start.7 = (bf16[32,6,16,128]{3,2,1,0:T(8,128)(2,1)S(1)}, bf16[32,6,16,128]{3,2,1,0:T(8,128)(2,1)}, u32[]{:S(2)}) copy-start(bf16[32,6,16,128]{3,2,1,0:T(8,128)(2,1)} %get-tuple-element.41) | copy-start | bytes 2359300
  142.0 4.2 %copy-start.9 = (bf16[192,768]{1,0:T(8,128)(2,1)}, bf16[192,768]{1,0:T(8,128)(2,1)S(1)}, u32[]{:S(2)}) copy-start(bf16[192,768]{1,0:T(8,128)(2,1)S(1)} %get-tuple-element.46) | copy-start | bytes 884740
  142.0 8.2 %copy-start.11 = (bf16[192,768]{1,0:T(8,128)(2,1)}, bf16[192,768]{1,0:T(8,128)(2,1)S(1)}, u32[]{:S(2)}) copy-start(bf16[192,768]{1,0:T(8,128)(2,1)S(1)} %get-tuple-element.39) | copy-start | bytes 884740
  142.0 4.2 %copy-start.6 = (bf16[32,6,16,128]{3,2,1,0:T(8,128)(2,1)S(1)}, bf16[32,6,16,128]{3,2,1,0:T(8,128)(2,1)}, u32[]{:S(2)}) copy-start(bf16[32,6,16,128]{3,2,1,0:T(8,128)(2,1)} %copy-done.5) | copy-start | bytes 2359300
  142.0 8.1 %slice-start = ((s8[6291456]{0:T(1024)(128)(4,1)}), s8[4194304]{0:T(1024)(128)(4,1)S(1)}, s32[]{:S(2)}) async-start(s8[6291456]{0:T(1024)(128)(4,1)} %bitcast.154), calls=%async_computation.6 | async-start | bytes 8388608
  146.2 4.0 %slice-start.1 = ((s8[6291456]{0:T(1024)(128)(4,1)}), s8[2097152]{0:T(1024)(128)(4,1)S(1)}, s32[]{:S(2)}) async-start(s8[6291456]{0:T(1024)(128)(4,1)} %bitcast.154), calls=%async_computation.7 | async-start | bytes 4194304
  156.1 2.2 copy-start.3
  160.9 8.2 %copy-start.10 = (bf16[192,768]{1,0:T(8,128)(2,1)S(1)}, bf16[192,768]{1,0:T(8,128)(2,1)}, u32[]{:S(2)}) copy-start(bf16[192,768]{1,0:T(8,128)(2,1)} %copy-done.9) | copy-start | bytes 884740
  160.9 32.2 %all-to-all-start.1 = ((bf16[32,8,16,128]{3,2,1,0:T(8,128)(2,1)}), bf16[32,8,16,128]{3,2,1,0:T(8,128)(2,1)}, u32[]{:S(2)}, u32[]{:S(2)}) async-start(bf16[32,8,16,128]{3,2,1,0:T(8,128)(2,1)} %fusion.40), calls=%async_computation.1 | async-start | bytes 2097152 | tf_op jit(solution)/shard_map/all_to_all | solution.py:119
  166.8 2.3 copy-start.4
  170.3 28.4 %copy-start.19 = (s32[48,8]{0,1:T(8,128)S(1)}, s32[48,8]{0,1:T(8,128)}, u32[]{:S(2)}) copy-start(s32[48,8]{0,1:T(8,128)} %param.10) | copy-start | bytes 4612
  170.3 28.6 %copy-start.18 = (s32[384]{0:T(512)S(1)}, s32[384]{0:T(512)}, u32[]{:S(2)}) copy-start(s32[384]{0:T(512)} %copy-done.17) | copy-start | bytes 4612
  170.3 53.0 %copy-start.16 = (s32[384]{0:T(512)S(1)}, s32[384]{0:T(512)}, u32[]{:S(2)}) copy-start(s32[384]{0:T(512)} %copy-done.15) | copy-start | bytes 4612
  193.1 29.1 %all-to-all-start.3 = ((bf16[32,7,16,128]{3,2,1,0:T(8,128)(2,1)}), bf16[32,7,16,128]{3,2,1,0:T(8,128)(2,1)}, u32[]{:S(2)}, u32[]{:S(2)}) async-start(bf16[32,7,16,128]{3,2,1,0:T(8,128)(2,1)} %fusion.41), calls=%async_computation.3 | async-start | bytes 1835008 | tf_op jit(solution)/shard_map/all_to_all | solution.py:119
  (4 other events, 3.6 us)
Sparse Core Ops, SparseCore 0:
  156.1 56.6 reduce-scatter.1

commit v4 on v2

--- a/solution.py
+++ b/solution.py
@@ -27,7 +27,7 @@
     return jnp.where(values < 0, -rounded, rounded).astype(jnp.bfloat16)
 
 
-def body(tokens, grad_out, expert_ids, combine, w_gate, w_up, w_down, dither_keys):
+def layer(tokens, grad_out, expert_ids, combine, w_gate, w_up, w_down, dither_keys):
     tok_dev, model_width = tokens.shape
     fan_out = expert_ids.shape[1]
     owners = lax.axis_size("expert")
@@ -93,15 +93,6 @@
     ).astype(jnp.bfloat16)
     up_rows_grad = (hidden_grad * silu_val).astype(jnp.bfloat16)
     scaled_grad = (weight * row_g.astype(jnp.float32)).astype(jnp.bfloat16)
-    gate_part = jnp.dot(row_x.T, gate_rows_grad, preferred_element_type=jnp.float32)
-    up_part = jnp.dot(row_x.T, up_rows_grad, preferred_element_type=jnp.float32)
-    down_part_t = jnp.dot(scaled_grad.T, hidden, preferred_element_type=jnp.float32)
-    hidden_units = gate_w.shape[1]
-    parts = jnp.concatenate(
-        [gate_part.astype(jnp.bfloat16), up_part.astype(jnp.bfloat16), down_part_t.astype(jnp.bfloat16)],
-        axis=1,
-    )
-    reduced = lax.psum_scatter(parts, "dp", scatter_dimension=0, tiled=True)
     row_grad = (
         jnp.dot(gate_rows_grad, gate_w.T, preferred_element_type=jnp.float32)
         + jnp.dot(up_rows_grad, up_w.T, preferred_element_type=jnp.float32)
@@ -113,14 +104,26 @@
         [row_grad.reshape(owners, capacity, tile_rows, lanes), comb_tile], axis=1
     )
     back = lax.all_to_all(back_send, "expert", split_axis=0, concat_axis=0, tiled=True)
-    back_rows = back[:, :capacity].reshape(slot_count, tile_rows, lanes)
-    back_comb = back[:, capacity, 0, :capacity].reshape(slot_count)
+    gate_part = jnp.dot(row_x.T, gate_rows_grad, preferred_element_type=jnp.float32)
+    up_part = jnp.dot(row_x.T, up_rows_grad, preferred_element_type=jnp.float32)
+    down_part_t = jnp.dot(scaled_grad.T, hidden, preferred_element_type=jnp.float32)
+    parts = jnp.concatenate(
+        [gate_part.astype(jnp.bfloat16), up_part.astype(jnp.bfloat16), down_part_t.astype(jnp.bfloat16)],
+        axis=1,
+    )
+    hidden_units = gate_w.shape[1]
+    reduced = lax.psum_scatter(parts, "dp", scatter_dimension=0, tiled=True)
+    dest = slot_index // capacity
+    back_rows = back.reshape(owners * (capacity + 1), tile_rows, lanes)[slot_index + dest]
     grad_tokens = (
-        jnp.sum(back_rows[slot_index].reshape(tok_dev, fan_out, tile_rows, lanes).astype(jnp.float32), axis=1)
+        jnp.sum(back_rows.reshape(tok_dev, fan_out, tile_rows, lanes).astype(jnp.float32), axis=1)
         .astype(jnp.bfloat16)
         .reshape(tok_dev, model_width)
     )
-    grad_combine = back_comb[slot_index].reshape(tok_dev, fan_out)
+    back_comb = back[:, capacity, 0, :capacity].reshape(slot_count).astype(jnp.float32)
+    grad_combine = (
+        jnp.sum(jnp.where(hit, back_comb[None, :], 0.0), axis=1).astype(jnp.bfloat16).reshape(tok_dev, fan_out)
+    )
     gate_grad = reduced[:, :hidden_units]
     up_grad = reduced[:, hidden_units : 2 * hidden_units]
     down_grad = reduced[:, 2 * hidden_units :].T
@@ -135,7 +138,7 @@
 
 def solution(mesh):
     return jax.shard_map(
-        body,
+        layer,
         mesh=mesh,
         in_specs=(
             P(("dp", "expert"), None),

time: 223 us -> 217 us (0.973)
  local copies, waits for them, and re-layouts: 31.1 us -> 24.5 us
    slice x5 -> x3, local copies, waits for them, and re-layouts: 7.18 us -> 3.31 us  [the longest x1 1.77 us: layer(): row_x = wire[:, :capacity].reshape(slot_count, model_width)]
    gather x3 -> x2, local copies, waits for them, and re-layouts: 10.6 us -> 7.87 us  [the longest x1 4.29 us: layer(): table[tile_index]]
  transfers between devices with their start and end apart: 2 -> 2, of which waited for: 1 -> 1; matrix products, arithmetic and copies ran while one was open for 9% -> 7% of each run, Pallas kernels for 0% -> 0%
where the time goes in v4:
time: 217 us
  blocking collectives  93.1 us (43%)
  waiting for transfers between devices  43.8 us (20%)
  local copies, waits for them, and re-layouts  24.5 us (11%)
  matrix products  20.4 us (9%)
  between operations  15.6 us (7%)
  other arithmetic  13.1 us (6%)
  starting transfers between devices  6.07 us (3%)
    all_to_all x1, blocking collectives, layer(): lax.all_to_all(table[tile_index], 'expert', split_axis=0, concat_axis=0,...  93.1 us
    all_to_all x1, waiting for transfers between devices, layer(): lax.all_to_all(back_send, 'expert', split_axis=0, concat_axis=0, tiled=True)  43.8 us
    unnamed x34, local copies, waits for them, and re-layouts  8.97 us
    all_to_all x1, starting transfers between devices, layer(): lax.all_to_all(back_send, 'expert', split_axis=0, concat_axis=0, tiled=True)  6.03 us
    dot_general x1, matrix products, layer(): back_grad = jnp.dot(row_g, down_w.T, preferred_element_type=jnp.float32)  5.39 us
    concatenate x1, other arithmetic, layer(): jnp.concatenate([gate_part.astype(jnp.bfloat16), up_part.astype(jnp.bfloa...  4.48 us
  transfers between devices with their start and end apart: 2, of which 1 were waited for; matrix products, arithmetic and copies ran while one was open for 7% of the time, Pallas kernels for 0%

profile of v4, /device:TPU:8, one launch (start us, length us, event | category | flops | bytes accessed | tf_op | source)
XLA Modules:
  0.0 216.6 jit_solution(10126877427692151570)
XLA Ops:
  7.2 0.9 copy.38
  9.9 1.3 fusion.82
  12.6 2.7 %fusion.69 = (bf16[6,8,16,128]{3,1,2,0:T(8,128)(2,1)S(1)}, bf16[6,8,16,128]{3,1,2,0:T(8,128)(2,1)S(1)}) fusion(bf16[48,2048]{1,0:T(8,128)(2,1)} %param.9, s32[]{:T(128)S(6)} %xor.58, s32[48]{0:T(128)S(1)} %add_multiply_fusion, s32[]{:T(128)S(6)} %xor.50, bf16[48,2048]{1,0:T(8,128)(2,1)} %param.8), kind=kLoop, calls=%fused_computation.119 | loop fusion | flops 13074432 | bytes 786632
  19.4 4.3 %gather_fusion = bf16[864,16,128]{2,1,0:T(8,128)(2,1)} fusion(bf16[130,16,128]{2,1,0:T(8,128)(2,1)} %pad_dynamic-update-slice_fusion, s32[1024]{0:T(1024)S(1)} %pad_clamp_fusion.1), kind=kCustom, calls=%fused_computation | custom fusion | bytes 7081344 | tf_op jit(solution)/shard_map/gather | solution.py:76
  23.7 93.1 %all_to_all.10 = bf16[32,27,16,128]{3,2,1,0:T(8,128)(2,1)S(1)} all-to-all(bf16[32,27,16,128]{3,2,1,0:T(8,128)(2,1)} %bitcast.93), channel_id=1, replica_groups=mesh['dp'=8,'expert'=32] {'expert'}, dimensions={0} | all-to-all | bytes 7077888 | tf_op jit(solution)/shard_map/all_to_all | solution.py:76
  116.8 1.8 fusion.81
  119.3 2.5 %fusion.7 = f32[416,768]{1,0:T(8,128)} fusion(bf16[1,2048,768]{2,1,0:T(8,128)(2,1)S(1)} %copy-done.6, bf16[52,8,16,128]{3,2,1,0:T(8,128)(2,1)S(1)} %bitcast.96), kind=kOutput, calls=%fused_computation.16 | convolution fusion | flops 1308622848 | bytes 6127616 | tf_op jit(solution)/shard_map/dot_general | solution.py:84
  121.9 2.6 %fusion.3 = f32[416,768]{1,0:T(8,128)} fusion(bf16[1,2048,768]{2,1,0:T(8,128)(2,1)S(1)} %copy-done, bf16[52,8,16,128]{3,2,1,0:T(8,128)(2,1)S(1)} %bitcast.97), kind=kOutput, calls=%fused_computation.12 | convolution fusion | flops 1308622848 | bytes 6127616 | tf_op jit(solution)/shard_map/dot_general | solution.py:83
  124.6 5.4 %multiply_reduce_fusion = (bf16[416]{0:T(512)(128)(2,1)S(1)}, bf16[416,768]{1,0:T(8,128)(2,1)S(1)}, bf16[416,768]{1,0:T(8,128)(2,1)S(1)}, bf16[416,768]{1,0:T(8,128)(2,1)S(1)}) fusion(f32[416,768]{1,0:T(8,128)} %fusion.7, f32[416,768]{1,0:T(8,128)} %fusion.3, f32[416]{0:T(512)S(1)} %reshape.315, bf16[1,768,2048]{2,1,0:T(8,128)(2,1)} %param.14, ...), kind=kOutput, calls=%fused_computation.31 | convolution fusion | flops 1314692736 | bytes 9324992 | tf_op jit(solution)/shard_map/dot_general | solution.py:88
  130.0 2.0 convolution_convert_fusion
  132.0 1.9 convolution_convert_fusion.1
  133.9 1.9 convolution_convert_fusion.2
  135.7 4.5 %pad_maximum_fusion = bf16[2048,2304]{0,1:T(8,128)(2,1)} fusion(bf16[2048,768]{0,1:T(8,128)(2,1)S(1)} %convolution_convert_fusion, bf16[2048,768]{0,1:T(8,128)(2,1)S(1)} %convolution_convert_fusion.1, bf16[2048,768]{0,1:T(8,128)(2,1)S(1)} %convolution_convert_fusion.2), kind=kLoop, calls=%fused_computation.2 | loop fusion | flops 28311552 | bytes 18874368 | tf_op jit(solution)/shard_map/concatenate | solution.py:110
  140.4 2.7 %fusion.1 = f32[416,2048]{1,0:T(8,128)S(1)} fusion(bf16[416,768]{1,0:T(8,128)(2,1)} %copy-done.8, bf16[1,2048,768]{2,1,0:T(8,128)(2,1)S(1)} %copy-done), kind=kOutput, calls=%fused_computation.10 | convolution fusion | flops 1308622848 | bytes 7192576 | tf_op jit(solution)/shard_map/dot_general | solution.py:97
  143.1 1.5 fusion.21
  145.1 1.6 fusion.13
  146.7 6.0 %all-to-all-start.1 = ((bf16[32,14,16,128]{3,2,1,0:T(8,128)(2,1)}), bf16[32,14,16,128]{3,2,1,0:T(8,128)(2,1)}, u32[]{:S(2)}, u32[]{:S(2)}) async-start(bf16[32,14,16,128]{3,2,1,0:T(8,128)(2,1)} %fusion.13), calls=%async_computation.1 | async-start | bytes 3670016 | tf_op jit(solution)/shard_map/all_to_all | solution.py:106
  153.0 43.8 %all-to-all-done.1 = bf16[32,14,16,128]{3,2,1,0:T(8,128)(2,1)} async-done(((bf16[32,14,16,128]{3,2,1,0:T(8,128)(2,1)}), bf16[32,14,16,128]{3,2,1,0:T(8,128)(2,1)}, u32[]{:S(2)}, u32[]{:S(2)}) %all-to-all-start.1) | async-done | bytes 1835040 | tf_op jit(solution)/shard_map/all_to_all | solution.py:106
  196.8 3.6 %gather_fusion.1 = bf16[384,16,128]{2,1,0:T(8,128)(2,1)} fusion(bf16[448,16,128]{2,1,0:T(8,128)(2,1)} %bitcast.8, s32[1024]{0:T(1024)S(1)} %pad_clamp_fusion), kind=kCustom, calls=%fused_computation.1 | custom fusion | bytes 3147264 | tf_op jit(solution)/shard_map/gather | solution.py:117
  200.4 1.7 reduce_sum.54
  202.8 0.9 fusion.74
  204.7 2.2 %slice_bitcast_fusion = (bf16[1,768,256]{2,1,0:T(8,128)(2,1)}, bf16[1,256,768]{1,2,0:T(8,128)(2,1)S(1)}, bf16[1,256,768]{1,2,0:T(8,128)(2,1)}) fusion(bf16[256,2304]{0,1:T(8,128)(2,1)} %reduce-scatter.2.cloned.1.call-done), kind=kLoop, calls=%fused_computation.113 | loop fusion | bytes 2359296 | tf_op jit(solution)/shard_map/broadcast_in_dim | solution.py:135
  206.9 1.9 copy.47
  208.8 0.9 copy.48
  (69 shorter events, 9.3 us)
Async XLA Ops:
  7.2 114.7 %copy-start = (bf16[1,2048,768]{2,1,0:T(8,128)(2,1)S(1)}, bf16[1,2048,768]{2,1,0:T(8,128)(2,1)}, u32[]{:S(2)}) copy-start(bf16[1,2048,768]{2,1,0:T(8,128)(2,1)} %param.12) | copy-start | bytes 9437188
  7.2 10.7 %copy-start.5 = (f32[48,8]{0,1:T(8,128)S(1)}, f32[48,8]{0,1:T(8,128)}, u32[]{:S(2)}) copy-start(f32[48,8]{0,1:T(8,128)} %param.11) | copy-start | bytes 4612
  7.2 197.5 %reduce-scatter.2.cloned.1.call-start = ((), (), s32[]{:S(2)}) async-start(), calls=%async_computation.3 | async-start | bytes 10616832 | tf_op jit(solution)/shard_map/reduce_scatter | solution.py:115
  116.8 2.5 %copy-start.6 = (bf16[1,2048,768]{2,1,0:T(8,128)(2,1)S(1)}, bf16[1,2048,768]{2,1,0:T(8,128)(2,1)}, u32[]{:S(2)}) copy-start(bf16[1,2048,768]{2,1,0:T(8,128)(2,1)} %param.13) | copy-start | bytes 9437188
  118.6 3.3 %copy-start.1 = (bf16[32,13,16,128]{3,2,1,0:T(8,128)(2,1)}, bf16[32,13,16,128]{3,2,1,0:T(8,128)(2,1)S(1)}, u32[]{:S(2)}) copy-start(bf16[32,13,16,128]{3,2,1,0:T(8,128)(2,1)S(1)} %get-tuple-element.28) | copy-start | bytes 5111812
  124.6 5.4 %copy-start.3 = (bf16[32,13,16,128]{3,2,1,0:T(8,128)(2,1)S(1)}, bf16[32,13,16,128]{3,2,1,0:T(8,128)(2,1)}, u32[]{:S(2)}) copy-start(bf16[32,13,16,128]{3,2,1,0:T(8,128)(2,1)} %get-tuple-element.29) | copy-start | bytes 5111812
  130.0 2.0 copy-start.9
  130.0 3.9 %copy-start.8 = (bf16[416,768]{1,0:T(8,128)(2,1)}, bf16[416,768]{1,0:T(8,128)(2,1)S(1)}, u32[]{:S(2)}) copy-start(bf16[416,768]{1,0:T(8,128)(2,1)S(1)} %get-tuple-element.27) | copy-start | bytes 1916932
  130.0 2.0 copy-start.2
  140.4 2.8 %copy-start.7 = (bf16[1,2048,768]{2,1,0:T(8,128)(2,1)S(1)}, bf16[1,2048,768]{2,1,0:T(8,128)(2,1)}, u32[]{:S(2)}) copy-start(bf16[1,2048,768]{2,1,0:T(8,128)(2,1)} %param.13) | copy-start | bytes 9437188
  140.4 2.8 %copy-start.10 = (bf16[416,768]{1,0:T(8,128)(2,1)S(1)}, bf16[416,768]{1,0:T(8,128)(2,1)}, u32[]{:S(2)}) copy-start(bf16[416,768]{1,0:T(8,128)(2,1)} %copy-done.9) | copy-start | bytes 1916932
  146.7 6.0 %copy-start.4 = (s32[48,8]{0,1:T(8,128)S(1)}, s32[48,8]{0,1:T(8,128)}, u32[]{:S(2)}) copy-start(s32[48,8]{0,1:T(8,128)} %param.10) | copy-start | bytes 4612
  146.7 50.1 %all-to-all-start.1 = ((bf16[32,14,16,128]{3,2,1,0:T(8,128)(2,1)}), bf16[32,14,16,128]{3,2,1,0:T(8,128)(2,1)}, u32[]{:S(2)}, u32[]{:S(2)}) async-start(bf16[32,14,16,128]{3,2,1,0:T(8,128)(2,1)} %fusion.13), calls=%async_computation.1 | async-start | bytes 3670016 | tf_op jit(solution)/shard_map/all_to_all | solution.py:106
Sparse Core Ops, SparseCore 0:
  140.4 56.6 reduce-scatter.1

commit v5 on v4

--- a/solution.py
+++ b/solution.py
@@ -27,7 +27,7 @@
     return jnp.where(values < 0, -rounded, rounded).astype(jnp.bfloat16)
 
 
-def layer(tokens, grad_out, expert_ids, combine, w_gate, w_up, w_down, dither_keys):
+def body(tokens, grad_out, expert_ids, combine, w_gate, w_up, w_down, dither_keys):
     tok_dev, model_width = tokens.shape
     fan_out = expert_ids.shape[1]
     owners = lax.axis_size("expert")
@@ -107,12 +107,10 @@
     gate_part = jnp.dot(row_x.T, gate_rows_grad, preferred_element_type=jnp.float32)
     up_part = jnp.dot(row_x.T, up_rows_grad, preferred_element_type=jnp.float32)
     down_part_t = jnp.dot(scaled_grad.T, hidden, preferred_element_type=jnp.float32)
-    parts = jnp.concatenate(
-        [gate_part.astype(jnp.bfloat16), up_part.astype(jnp.bfloat16), down_part_t.astype(jnp.bfloat16)],
-        axis=1,
+    parts = jnp.stack(
+        [gate_part.astype(jnp.bfloat16), up_part.astype(jnp.bfloat16), down_part_t.astype(jnp.bfloat16)]
     )
-    hidden_units = gate_w.shape[1]
-    reduced = lax.psum_scatter(parts, "dp", scatter_dimension=0, tiled=True)
+    reduced = lax.psum_scatter(parts, "dp", scatter_dimension=1, tiled=True)
     dest = slot_index // capacity
     back_rows = back.reshape(owners * (capacity + 1), tile_rows, lanes)[slot_index + dest]
     grad_tokens = (
@@ -124,9 +122,9 @@
     grad_combine = (
         jnp.sum(jnp.where(hit, back_comb[None, :], 0.0), axis=1).astype(jnp.bfloat16).reshape(tok_dev, fan_out)
     )
-    gate_grad = reduced[:, :hidden_units]
-    up_grad = reduced[:, hidden_units : 2 * hidden_units]
-    down_grad = reduced[:, 2 * hidden_units :].T
+    gate_grad = reduced[0]
+    up_grad = reduced[1]
+    down_grad = reduced[2].T
     return (
         grad_tokens,
         grad_combine,
@@ -138,7 +136,7 @@
 
 def solution(mesh):
     return jax.shard_map(
-        layer,
+        body,
         mesh=mesh,
         in_specs=(
             P(("dp", "expert"), None),

time: 217 us -> 216 us (level)
    another operation x2 -> x3, other arithmetic: 0.92 us -> 5.55 us  [the longest x1 4.63 us: body(): jnp.stack([gate_part.astype(jnp.bfloat16), up_part.astype(jnp.bfloat16),...]
    concatenate x3 -> x2, other arithmetic: 6.08 us -> 1.6 us  [the longest x1 1.6 us: body(): jnp.concatenate([row_grad.reshape(owners, capacity, tile_rows, lanes), co...]
    unnamed x34 -> x33, local copies, waits for them, and re-layouts: 8.97 us -> 7.06 us
where the time goes in v5:
time: 216 us; the launch traced here: 215 us
  blocking collectives  93.1 us (43%)
  waiting for transfers between devices  43.8 us (20%)
  local copies, waits for them, and re-layouts  22.6 us (10%)
  matrix products  20.6 us (10%)
  between operations  15.6 us (7%)
  other arithmetic  13.2 us (6%)
  starting transfers between devices  6.07 us (3%)
    all_to_all x1, blocking collectives, body(): lax.all_to_all(table[tile_index], 'expert', split_axis=0, concat_axis=0,...  93.1 us
    all_to_all x1, waiting for transfers between devices, body(): lax.all_to_all(back_send, 'expert', split_axis=0, concat_axis=0, tiled=True)  43.7 us
    unnamed x33, local copies, waits for them, and re-layouts  7.06 us
    all_to_all x1, starting transfers between devices, body(): lax.all_to_all(back_send, 'expert', split_axis=0, concat_axis=0, tiled=True)  6.03 us
    dot_general x1, matrix products, body(): back_grad = jnp.dot(row_g, down_w.T, preferred_element_type=jnp.float32)  5.39 us
    another operation x1, other arithmetic, body(): jnp.stack([gate_part.astype(jnp.bfloat16), up_part.astype(jnp.bfloat16),...  4.63 us
  transfers between devices with their start and end apart: 2, of which 1 were waited for; matrix products, arithmetic and copies ran while one was open for 7% of the time, Pallas kernels for 0%

profile of v5, /device:TPU:8, one launch (start us, length us, event | category | flops | bytes accessed | tf_op | source)
XLA Modules:
  0.0 215.0 jit_solution(14925793877921204030)
XLA Ops:
  7.2 0.9 copy.35
  8.4 0.9 reduce-window.6
  9.9 1.3 fusion.85
  12.6 2.7 %fusion.72 = (bf16[6,8,16,128]{3,1,2,0:T(8,128)(2,1)S(1)}, bf16[6,8,16,128]{3,1,2,0:T(8,128)(2,1)S(1)}) fusion(bf16[48,2048]{1,0:T(8,128)(2,1)} %param.9, s32[]{:T(128)S(6)} %xor.58, s32[48]{0:T(128)S(1)} %add_multiply_fusion, s32[]{:T(128)S(6)} %xor.50, bf16[48,2048]{1,0:T(8,128)(2,1)} %param.8), kind=kLoop, calls=%fused_computation.120 | loop fusion | flops 13074432 | bytes 786632
  19.4 4.3 %gather_fusion = bf16[864,16,128]{2,1,0:T(8,128)(2,1)} fusion(bf16[130,16,128]{2,1,0:T(8,128)(2,1)} %pad_dynamic-update-slice_fusion, s32[1024]{0:T(1024)S(1)} %pad_clamp_fusion.1), kind=kCustom, calls=%fused_computation | custom fusion | bytes 7081344 | tf_op jit(solution)/shard_map/gather | solution.py:76
  23.7 93.1 %all_to_all.10 = bf16[32,27,16,128]{3,2,1,0:T(8,128)(2,1)S(1)} all-to-all(bf16[32,27,16,128]{3,2,1,0:T(8,128)(2,1)} %bitcast.97), channel_id=1, replica_groups=mesh['dp'=8,'expert'=32] {'expert'}, dimensions={0} | all-to-all | bytes 7077888 | tf_op jit(solution)/shard_map/all_to_all | solution.py:76
  116.8 1.8 fusion.84
  119.3 2.5 %fusion.7 = f32[416,768]{1,0:T(8,128)} fusion(bf16[1,2048,768]{2,1,0:T(8,128)(2,1)S(1)} %copy-done.6, bf16[52,8,16,128]{3,2,1,0:T(8,128)(2,1)S(1)} %bitcast.100), kind=kOutput, calls=%fused_computation.16 | convolution fusion | flops 1308622848 | bytes 6127616 | tf_op jit(solution)/shard_map/dot_general | solution.py:84
  121.9 2.6 %fusion.3 = f32[416,768]{1,0:T(8,128)} fusion(bf16[1,2048,768]{2,1,0:T(8,128)(2,1)S(1)} %copy-done, bf16[52,8,16,128]{3,2,1,0:T(8,128)(2,1)S(1)} %bitcast.101), kind=kOutput, calls=%fused_computation.12 | convolution fusion | flops 1308622848 | bytes 6127616 | tf_op jit(solution)/shard_map/dot_general | solution.py:83
  124.6 5.4 %multiply_reduce_fusion = (bf16[416]{0:T(512)(128)(2,1)S(1)}, bf16[416,768]{1,0:T(8,128)(2,1)S(1)}, bf16[416,768]{1,0:T(8,128)(2,1)S(1)}, bf16[416,768]{1,0:T(8,128)(2,1)S(1)}) fusion(f32[416,768]{1,0:T(8,128)} %fusion.7, f32[416,768]{1,0:T(8,128)} %fusion.3, f32[416]{0:T(512)S(1)} %reshape.315, bf16[1,768,2048]{2,1,0:T(8,128)(2,1)} %param.14, ...), kind=kOutput, calls=%fused_computation.34 | convolution fusion | flops 1314692736 | bytes 9324992 | tf_op jit(solution)/shard_map/dot_general | solution.py:88
  130.0 2.1 fusion.13
  132.2 1.9 fusion.12
  134.1 1.9 fusion.11
  136.0 4.6 %pad_maximum_fusion = bf16[3,2048,768]{2,1,0:T(8,128)(2,1)} fusion(bf16[1,2048,768]{2,1,0:T(8,128)(2,1)S(1)} %fusion.13, bf16[1,2048,768]{2,1,0:T(8,128)(2,1)S(1)} %fusion.12, bf16[1,2048,768]{2,1,0:T(8,128)(2,1)S(1)} %fusion.11), kind=kLoop, calls=%fused_computation.2 | loop fusion | flops 9437184 | bytes 18874368 | tf_op jit(solution)/shard_map/stack | solution.py:110
  140.7 2.7 %fusion.1 = f32[416,2048]{1,0:T(8,128)S(1)} fusion(bf16[416,768]{1,0:T(8,128)(2,1)} %copy-done.8, bf16[1,2048,768]{2,1,0:T(8,128)(2,1)S(1)} %copy-done), kind=kOutput, calls=%fused_computation.10 | convolution fusion | flops 1308622848 | bytes 7192576 | tf_op jit(solution)/shard_map/dot_general | solution.py:97
  143.5 1.5 fusion.24
  145.5 1.6 fusion.16
  147.1 6.0 %all-to-all-start.1 = ((bf16[32,14,16,128]{3,2,1,0:T(8,128)(2,1)}), bf16[32,14,16,128]{3,2,1,0:T(8,128)(2,1)}, u32[]{:S(2)}, u32[]{:S(2)}) async-start(bf16[32,14,16,128]{3,2,1,0:T(8,128)(2,1)} %fusion.16), calls=%async_computation.1 | async-start | bytes 3670016 | tf_op jit(solution)/shard_map/all_to_all | solution.py:106
  153.4 43.7 %all-to-all-done.1 = bf16[32,14,16,128]{3,2,1,0:T(8,128)(2,1)} async-done(((bf16[32,14,16,128]{3,2,1,0:T(8,128)(2,1)}), bf16[32,14,16,128]{3,2,1,0:T(8,128)(2,1)}, u32[]{:S(2)}, u32[]{:S(2)}) %all-to-all-start.1) | async-done | bytes 1835040 | tf_op jit(solution)/shard_map/all_to_all | solution.py:106
  197.1 3.6 %gather_fusion.1 = bf16[384,16,128]{2,1,0:T(8,128)(2,1)} fusion(bf16[448,16,128]{2,1,0:T(8,128)(2,1)} %bitcast.8, s32[1024]{0:T(1024)S(1)} %pad_clamp_fusion), kind=kCustom, calls=%fused_computation.1 | custom fusion | bytes 3147264 | tf_op jit(solution)/shard_map/gather | solution.py:115
  200.7 1.7 reduce_sum.54
  203.1 0.9 fusion.77
  205.1 2.2 %slice_bitcast_fusion = (bf16[1,768,256]{1,2,0:T(8,128)(2,1)S(1)}, bf16[1,256,768]{2,1,0:T(8,128)(2,1)}, bf16[1,256,768]{2,1,0:T(8,128)(2,1)}) fusion(bf16[3,256,768]{2,1,0:T(8,128)(2,1)} %reduce-scatter.2.cloned.1.call-done), kind=kLoop, calls=%fused_computation.116 | loop fusion | bytes 2359296 | tf_op jit(solution)/shard_map/broadcast_in_dim | solution.py:133
  207.2 0.9 copy.44
  (68 shorter events, 8.5 us)
Async XLA Ops:
  7.2 114.7 %copy-start = (bf16[1,2048,768]{2,1,0:T(8,128)(2,1)S(1)}, bf16[1,2048,768]{2,1,0:T(8,128)(2,1)}, u32[]{:S(2)}) copy-start(bf16[1,2048,768]{2,1,0:T(8,128)(2,1)} %param.12) | copy-start | bytes 9437188
  7.2 10.7 %copy-start.5 = (f32[48,8]{0,1:T(8,128)S(1)}, f32[48,8]{0,1:T(8,128)}, u32[]{:S(2)}) copy-start(f32[48,8]{0,1:T(8,128)} %param.11) | copy-start | bytes 4612
  7.2 197.9 %reduce-scatter.2.cloned.1.call-start = ((), (), s32[]{:S(2)}) async-start(), calls=%async_computation.3 | async-start | bytes 10616832 | tf_op jit(solution)/shard_map/reduce_scatter | solution.py:113
  116.8 2.5 %copy-start.6 = (bf16[1,2048,768]{2,1,0:T(8,128)(2,1)S(1)}, bf16[1,2048,768]{2,1,0:T(8,128)(2,1)}, u32[]{:S(2)}) copy-start(bf16[1,2048,768]{2,1,0:T(8,128)(2,1)} %param.13) | copy-start | bytes 9437188
  118.6 3.3 %copy-start.1 = (bf16[32,13,16,128]{3,2,1,0:T(8,128)(2,1)}, bf16[32,13,16,128]{3,2,1,0:T(8,128)(2,1)S(1)}, u32[]{:S(2)}) copy-start(bf16[32,13,16,128]{3,2,1,0:T(8,128)(2,1)S(1)} %get-tuple-element.28) | copy-start | bytes 5111812
  124.6 5.4 %copy-start.3 = (bf16[32,13,16,128]{3,2,1,0:T(8,128)(2,1)S(1)}, bf16[32,13,16,128]{3,2,1,0:T(8,128)(2,1)}, u32[]{:S(2)}) copy-start(bf16[32,13,16,128]{3,2,1,0:T(8,128)(2,1)} %get-tuple-element.29) | copy-start | bytes 5111812
  130.0 2.2 %copy-start.9 = (bf16[416,768]{1,0:T(8,128)(2,1)}, bf16[416,768]{1,0:T(8,128)(2,1)S(1)}, u32[]{:S(2)}) copy-start(bf16[416,768]{1,0:T(8,128)(2,1)S(1)} %get-tuple-element.30) | copy-start | bytes 1916932
  130.0 4.1 %copy-start.8 = (bf16[416,768]{1,0:T(8,128)(2,1)}, bf16[416,768]{1,0:T(8,128)(2,1)S(1)}, u32[]{:S(2)}) copy-start(bf16[416,768]{1,0:T(8,128)(2,1)S(1)} %get-tuple-element.27) | copy-start | bytes 1916932
  130.0 2.1 copy-start.2
  140.7 2.8 %copy-start.7 = (bf16[1,2048,768]{2,1,0:T(8,128)(2,1)S(1)}, bf16[1,2048,768]{2,1,0:T(8,128)(2,1)}, u32[]{:S(2)}) copy-start(bf16[1,2048,768]{2,1,0:T(8,128)(2,1)} %param.13) | copy-start | bytes 9437188
  140.7 2.8 %copy-start.10 = (bf16[416,768]{1,0:T(8,128)(2,1)S(1)}, bf16[416,768]{1,0:T(8,128)(2,1)}, u32[]{:S(2)}) copy-start(bf16[416,768]{1,0:T(8,128)(2,1)} %copy-done.9) | copy-start | bytes 1916932
  147.1 6.0 %copy-start.4 = (s32[48,8]{0,1:T(8,128)S(1)}, s32[48,8]{0,1:T(8,128)}, u32[]{:S(2)}) copy-start(s32[48,8]{0,1:T(8,128)} %param.10) | copy-start | bytes 4612
  147.1 50.0 %all-to-all-start.1 = ((bf16[32,14,16,128]{3,2,1,0:T(8,128)(2,1)}), bf16[32,14,16,128]{3,2,1,0:T(8,128)(2,1)}, u32[]{:S(2)}, u32[]{:S(2)}) async-start(bf16[32,14,16,128]{3,2,1,0:T(8,128)(2,1)} %fusion.16), calls=%async_computation.1 | async-start | bytes 3670016 | tf_op jit(solution)/shard_map/all_to_all | solution.py:106
Sparse Core Ops, SparseCore 0:
  140.7 56.6 reduce-scatter.1

commit v6 on v5

--- a/solution.py
+++ b/solution.py
@@ -112,12 +112,14 @@
     )
     reduced = lax.psum_scatter(parts, "dp", scatter_dimension=1, tiled=True)
     dest = slot_index // capacity
-    back_rows = back.reshape(owners * (capacity + 1), tile_rows, lanes)[slot_index + dest]
-    grad_tokens = (
-        jnp.sum(back_rows.reshape(tok_dev, fan_out, tile_rows, lanes).astype(jnp.float32), axis=1)
-        .astype(jnp.bfloat16)
-        .reshape(tok_dev, model_width)
-    )
+    returned = jnp.arange(owners * (capacity + 1), dtype=jnp.int32)
+    token_of = jnp.where(
+        (slot_index + dest)[None, :] == returned[:, None], (pair_rows // fan_out)[None, :], tok_dev
+    ).min(axis=1)
+    gather_matrix = (jnp.arange(tok_dev, dtype=jnp.int32)[:, None] == token_of[None, :]).astype(jnp.bfloat16)
+    grad_tokens = jnp.dot(
+        gather_matrix, back.reshape(owners * (capacity + 1), model_width), preferred_element_type=jnp.float32
+    ).astype(jnp.bfloat16)
     back_comb = back[:, capacity, 0, :capacity].reshape(slot_count).astype(jnp.float32)
     grad_combine = (
         jnp.sum(jnp.where(hit, back_comb[None, :], 0.0), axis=1).astype(jnp.bfloat16).reshape(tok_dev, fan_out)

time: 216 us -> 212 us (0.981)
  local copies, waits for them, and re-layouts: 22.6 us -> 18.1 us
  matrix products: 20.6 us -> 23.2 us
    gather x1 -> x0, local copies, waits for them, and re-layouts: 3.59 us -> none  [body(): back.reshape(owners * (capacity + 1), tile_rows, lanes)[slot_index + dest]]
    dot_general x0 -> x1, matrix products: none -> 2.61 us  [body(): jnp.dot(gather_matrix, back.reshape(owners * (capacity + 1), model_width)...]
    unnamed x33 -> x30, local copies, waits for them, and re-layouts: 7.06 us -> 6.32 us
  transfers between devices with their start and end apart: 2 -> 2, of which waited for: 1 -> 1; matrix products, arithmetic and copies ran while one was open for 7% -> 5% of each run, Pallas kernels for 0% -> 0%
where the time goes in v6:
time: 212 us
  blocking collectives  93.1 us (44%)
  waiting for transfers between devices  43.8 us (21%)
  matrix products  23.2 us (11%)
  local copies, waits for them, and re-layouts  18.1 us (9%)
  between operations  15.6 us (7%)
  other arithmetic  11.7 us (6%)
  starting transfers between devices  5.96 us (3%)
    all_to_all x1, blocking collectives, body(): lax.all_to_all(table[tile_index], 'expert', split_axis=0, concat_axis=0,...  93.1 us
    all_to_all x1, waiting for transfers between devices, body(): lax.all_to_all(back_send, 'expert', split_axis=0, concat_axis=0, tiled=True)  43.8 us
    unnamed x30, local copies, waits for them, and re-layouts  6.32 us
    all_to_all x1, starting transfers between devices, body(): lax.all_to_all(back_send, 'expert', split_axis=0, concat_axis=0, tiled=True)  5.93 us
    dot_general x1, matrix products, body(): back_grad = jnp.dot(row_g, down_w.T, preferred_element_type=jnp.float32)  5.39 us
    another operation x1, other arithmetic, body(): jnp.stack([gate_part.astype(jnp.bfloat16), up_part.astype(jnp.bfloat16),...  4.63 us
    gather x1, local copies, waits for them, and re-layouts, body(): table[tile_index]  4.29 us
  transfers between devices with their start and end apart: 2, of which 1 were waited for; matrix products, arithmetic and copies ran while one was open for 5% of the time, Pallas kernels for 0%

profile of v6, /device:TPU:8, one launch (start us, length us, event | category | flops | bytes accessed | tf_op | source)
XLA Modules:
  0.0 211.5 jit_solution(504335900110882025)
XLA Ops:
  7.2 0.9 copy.43
  8.4 0.9 reduce-window.6
  9.9 1.3 fusion.88
  12.6 2.7 %fusion.74 = (bf16[6,8,16,128]{3,1,2,0:T(8,128)(2,1)S(1)}, bf16[6,8,16,128]{3,1,2,0:T(8,128)(2,1)S(1)}) fusion(bf16[48,2048]{1,0:T(8,128)(2,1)} %param.9, s32[]{:T(128)S(6)} %xor.58, s32[48]{0:T(128)S(1)} %add_multiply_fusion, s32[]{:T(128)S(6)} %xor.50, bf16[48,2048]{1,0:T(8,128)(2,1)} %param.8), kind=kLoop, calls=%fused_computation.124 | loop fusion | flops 13074432 | bytes 786632
  19.4 4.3 %gather_fusion = bf16[864,16,128]{2,1,0:T(8,128)(2,1)} fusion(bf16[130,16,128]{2,1,0:T(8,128)(2,1)} %pad_dynamic-update-slice_fusion, s32[1024]{0:T(1024)S(1)} %pad_clamp_fusion), kind=kCustom, calls=%fused_computation | custom fusion | bytes 7081344 | tf_op jit(solution)/shard_map/gather | solution.py:76
  23.7 93.1 %all_to_all.10 = bf16[32,27,16,128]{3,2,1,0:T(8,128)(2,1)S(1)} all-to-all(bf16[32,27,16,128]{3,2,1,0:T(8,128)(2,1)} %bitcast.96), channel_id=1, replica_groups=mesh['dp'=8,'expert'=32] {'expert'}, dimensions={0} | all-to-all | bytes 7077888 | tf_op jit(solution)/shard_map/all_to_all | solution.py:76
  116.8 1.8 fusion.87
  118.6 0.7 copy-done.5
  119.3 2.5 %fusion.7 = f32[416,768]{1,0:T(8,128)} fusion(bf16[1,2048,768]{2,1,0:T(8,128)(2,1)S(1)} %copy-done.5, bf16[52,8,16,128]{3,2,1,0:T(8,128)(2,1)S(1)} %bitcast.98), kind=kOutput, calls=%fused_computation.15 | convolution fusion | flops 1308622848 | bytes 6127616 | tf_op jit(solution)/shard_map/dot_general | solution.py:84
  121.9 2.6 %fusion.3 = f32[416,768]{1,0:T(8,128)} fusion(bf16[1,2048,768]{2,1,0:T(8,128)(2,1)S(1)} %copy-done, bf16[52,8,16,128]{3,2,1,0:T(8,128)(2,1)S(1)} %bitcast.99), kind=kOutput, calls=%fused_computation.11 | convolution fusion | flops 1308622848 | bytes 6127616 | tf_op jit(solution)/shard_map/dot_general | solution.py:83
  124.6 5.4 %multiply_reduce_fusion = (bf16[416]{0:T(512)(128)(2,1)S(1)}, bf16[416,768]{1,0:T(8,128)(2,1)S(1)}, bf16[416,768]{1,0:T(8,128)(2,1)S(1)}, bf16[416,768]{1,0:T(8,128)(2,1)S(1)}) fusion(f32[416,768]{1,0:T(8,128)} %fusion.7, f32[416,768]{1,0:T(8,128)} %fusion.3, f32[416]{0:T(512)S(1)} %reshape.286, bf16[1,768,2048]{2,1,0:T(8,128)(2,1)} %param.14, ...), kind=kOutput, calls=%fused_computation.36 | convolution fusion | flops 1314692736 | bytes 9324992 | tf_op jit(solution)/shard_map/dot_general | solution.py:88
  130.0 2.1 fusion.13
  132.2 1.9 fusion.12
  134.1 1.9 fusion.11
  135.9 4.6 %pad_maximum_fusion = bf16[3,2048,768]{2,1,0:T(8,128)(2,1)} fusion(bf16[1,2048,768]{2,1,0:T(8,128)(2,1)S(1)} %fusion.13, bf16[1,2048,768]{2,1,0:T(8,128)(2,1)S(1)} %fusion.12, bf16[1,2048,768]{2,1,0:T(8,128)(2,1)S(1)} %fusion.11), kind=kLoop, calls=%fused_computation.1 | loop fusion | flops 9437184 | bytes 18874368 | tf_op jit(solution)/shard_map/stack | solution.py:110
  140.7 2.7 %fusion.1 = f32[416,2048]{1,0:T(8,128)S(1)} fusion(bf16[416,768]{1,0:T(8,128)(2,1)} %copy-done.7, bf16[1,2048,768]{2,1,0:T(8,128)(2,1)S(1)} %copy-done), kind=kOutput, calls=%fused_computation.9 | convolution fusion | flops 1308622848 | bytes 7192576 | tf_op jit(solution)/shard_map/dot_general | solution.py:97
  143.5 1.5 fusion.26
  145.5 1.6 fusion.16
  147.1 5.9 %all-to-all-start.1 = ((bf16[32,14,16,128]{3,2,1,0:T(8,128)(2,1)}), bf16[32,14,16,128]{3,2,1,0:T(8,128)(2,1)}, u32[]{:S(2)}, u32[]{:S(2)}) async-start(bf16[32,14,16,128]{3,2,1,0:T(8,128)(2,1)} %fusion.16), calls=%async_computation.1 | async-start | bytes 3670016 | tf_op jit(solution)/shard_map/all_to_all | solution.py:106
  153.2 43.8 %all-to-all-done.1 = bf16[32,14,16,128]{3,2,1,0:T(8,128)(2,1)} async-done(((bf16[32,14,16,128]{3,2,1,0:T(8,128)(2,1)}), bf16[32,14,16,128]{3,2,1,0:T(8,128)(2,1)}, u32[]{:S(2)}, u32[]{:S(2)}) %all-to-all-start.1) | async-done | bytes 1835040 | tf_op jit(solution)/shard_map/all_to_all | solution.py:106
  197.0 0.9 fusion.80
  198.9 2.6 %convolution_convert_fusion.3 = bf16[48,2048]{1,0:T(8,128)(2,1)} fusion(bf16[56,8,16,128]{3,2,1,0:T(8,128)(2,1)} %bitcast.33, s32[448]{0:T(512)S(1)} %select_reduce_fusion), kind=kOutput, calls=%fused_computation.22 | convolution fusion | flops 88200192 | bytes 2033408 | tf_op jit(solution)/shard_map/dot_general | solution.py:120
  201.6 2.2 %slice_bitcast_fusion = (bf16[1,768,256]{1,2,0:T(8,128)(2,1)S(1)}, bf16[1,256,768]{2,1,0:T(8,128)(2,1)}, bf16[1,256,768]{2,1,0:T(8,128)(2,1)}) fusion(bf16[3,256,768]{2,1,0:T(8,128)(2,1)} %reduce-scatter.2.cloned.1.call-done), kind=kLoop, calls=%fused_computation.120 | loop fusion | bytes 2359296 | tf_op jit(solution)/shard_map/broadcast_in_dim | solution.py:135
  203.7 0.9 copy.51
  (60 shorter events, 7.0 us)
Async XLA Ops:
  7.2 114.7 %copy-start = (bf16[1,2048,768]{2,1,0:T(8,128)(2,1)S(1)}, bf16[1,2048,768]{2,1,0:T(8,128)(2,1)}, u32[]{:S(2)}) copy-start(bf16[1,2048,768]{2,1,0:T(8,128)(2,1)} %param.12) | copy-start | bytes 9437188
  7.2 10.7 %copy-start.4 = (f32[48,8]{0,1:T(8,128)S(1)}, f32[48,8]{0,1:T(8,128)}, u32[]{:S(2)}) copy-start(f32[48,8]{0,1:T(8,128)} %param.11) | copy-start | bytes 4612
  7.2 194.4 %reduce-scatter.2.cloned.1.call-start = ((), (), s32[]{:S(2)}) async-start(), calls=%async_computation.3 | async-start | bytes 10616832 | tf_op jit(solution)/shard_map/reduce_scatter | solution.py:113
  116.8 2.5 %copy-start.5 = (bf16[1,2048,768]{2,1,0:T(8,128)(2,1)S(1)}, bf16[1,2048,768]{2,1,0:T(8,128)(2,1)}, u32[]{:S(2)}) copy-start(bf16[1,2048,768]{2,1,0:T(8,128)(2,1)} %param.13) | copy-start | bytes 9437188
  118.6 3.3 %copy-start.1 = (bf16[32,13,16,128]{3,2,1,0:T(8,128)(2,1)}, bf16[32,13,16,128]{3,2,1,0:T(8,128)(2,1)S(1)}, u32[]{:S(2)}) copy-start(bf16[32,13,16,128]{3,2,1,0:T(8,128)(2,1)S(1)} %get-tuple-element.35) | copy-start | bytes 5111812
  124.6 5.4 %copy-start.3 = (bf16[32,13,16,128]{3,2,1,0:T(8,128)(2,1)S(1)}, bf16[32,13,16,128]{3,2,1,0:T(8,128)(2,1)}, u32[]{:S(2)}) copy-start(bf16[32,13,16,128]{3,2,1,0:T(8,128)(2,1)} %get-tuple-element.36) | copy-start | bytes 5111812
  130.0 2.1 %copy-start.8 = (bf16[416,768]{1,0:T(8,128)(2,1)}, bf16[416,768]{1,0:T(8,128)(2,1)S(1)}, u32[]{:S(2)}) copy-start(bf16[416,768]{1,0:T(8,128)(2,1)S(1)} %get-tuple-element.37) | copy-start | bytes 1916932
  130.0 4.0 %copy-start.7 = (bf16[416,768]{1,0:T(8,128)(2,1)}, bf16[416,768]{1,0:T(8,128)(2,1)S(1)}, u32[]{:S(2)}) copy-start(bf16[416,768]{1,0:T(8,128)(2,1)S(1)} %get-tuple-element.34) | copy-start | bytes 1916932
  130.0 2.1 %copy-start.2 = (bf16[32,13,16,128]{3,2,1,0:T(8,128)(2,1)S(1)}, bf16[32,13,16,128]{3,2,1,0:T(8,128)(2,1)}, u32[]{:S(2)}) copy-start(bf16[32,13,16,128]{3,2,1,0:T(8,128)(2,1)} %copy-done.1) | copy-start | bytes 5111812
  140.7 2.8 %copy-start.6 = (bf16[1,2048,768]{2,1,0:T(8,128)(2,1)S(1)}, bf16[1,2048,768]{2,1,0:T(8,128)(2,1)}, u32[]{:S(2)}) copy-start(bf16[1,2048,768]{2,1,0:T(8,128)(2,1)} %param.13) | copy-start | bytes 9437188
  140.7 2.8 %copy-start.9 = (bf16[416,768]{1,0:T(8,128)(2,1)S(1)}, bf16[416,768]{1,0:T(8,128)(2,1)}, u32[]{:S(2)}) copy-start(bf16[416,768]{1,0:T(8,128)(2,1)} %copy-done.8) | copy-start | bytes 1916932
  147.1 49.9 %all-to-all-start.1 = ((bf16[32,14,16,128]{3,2,1,0:T(8,128)(2,1)}), bf16[32,14,16,128]{3,2,1,0:T(8,128)(2,1)}, u32[]{:S(2)}, u32[]{:S(2)}) async-start(bf16[32,14,16,128]{3,2,1,0:T(8,128)(2,1)} %fusion.16), calls=%async_computation.1 | async-start | bytes 3670016 | tf_op jit(solution)/shard_map/all_to_all | solution.py:106
Sparse Core Ops, SparseCore 0:
  140.7 56.7 reduce-scatter.1

commit v7 on v6

--- a/solution.py
+++ b/solution.py
@@ -104,12 +104,12 @@
         [row_grad.reshape(owners, capacity, tile_rows, lanes), comb_tile], axis=1
     )
     back = lax.all_to_all(back_send, "expert", split_axis=0, concat_axis=0, tiled=True)
-    gate_part = jnp.dot(row_x.T, gate_rows_grad, preferred_element_type=jnp.float32)
-    up_part = jnp.dot(row_x.T, up_rows_grad, preferred_element_type=jnp.float32)
-    down_part_t = jnp.dot(scaled_grad.T, hidden, preferred_element_type=jnp.float32)
-    parts = jnp.stack(
-        [gate_part.astype(jnp.bfloat16), up_part.astype(jnp.bfloat16), down_part_t.astype(jnp.bfloat16)]
-    )
+    parts = lax.dot_general(
+        jnp.stack([row_x, row_x, scaled_grad]),
+        jnp.stack([gate_rows_grad, up_rows_grad, hidden]),
+        (((1,), (1,)), ((0,), (0,))),
+        preferred_element_type=jnp.float32,
+    ).astype(jnp.bfloat16)
     reduced = lax.psum_scatter(parts, "dp", scatter_dimension=1, tiled=True)
     dest = slot_index // capacity
     returned = jnp.arange(owners * (capacity + 1), dtype=jnp.int32)

time: 212 us -> 228 us (1.075)
  local copies, waits for them, and re-layouts: 18.1 us -> 27.6 us
  matrix products: 23.2 us -> 27.4 us
  other arithmetic: 11.7 us -> 14.2 us
    dot_general x3 -> x1, matrix products: 5.86 us -> 11.7 us  [body(): lax.dot_general(jnp.stack([row_x, row_x, scaled_grad]), jnp.stack([gate_r...]
    convert_element_type x0 -> x2, other arithmetic: none -> 4.94 us  [body(): scaled_grad = (weight * row_g.astype(jnp.float32)).astype(jnp.bfloat16)]
    convert_element_type x0 -> x1, local copies, waits for them, and re-layouts: none -> 4.64 us  [body(): scaled_grad = (weight * row_g.astype(jnp.float32)).astype(jnp.bfloat16)]
    another operation x3 -> x2, other arithmetic: 5.55 us -> 0.92 us  [the longest x1 4.63 us: body(): jnp.stack([gate_part.astype(jnp.bfloat16), up_part.astype(jnp.bfloat16),...]
    another operation x0 -> x1, local copies, waits for them, and re-layouts: none -> 3.8 us  [body(): jnp.stack([row_x, row_x, scaled_grad])]
    unnamed x30 -> x28, local copies, waits for them, and re-layouts: 6.32 us -> 9.21 us
  transfers between devices with their start and end apart: 2 -> 2, of which waited for: 1 -> 1; matrix products, arithmetic and copies ran while one was open for 5% -> 6% of each run, Pallas kernels for 0% -> 0%
where the time goes in v7:
time: 228 us
  blocking collectives  93.1 us (41%)
  waiting for transfers between devices  43.7 us (19%)
  local copies, waits for them, and re-layouts  27.6 us (12%)
  matrix products  27.4 us (12%)
  between operations  15.6 us (7%)
  other arithmetic  14.2 us (6%)
  starting transfers between devices  6.09 us (3%)
    all_to_all x1, blocking collectives, body(): lax.all_to_all(table[tile_index], 'expert', split_axis=0, concat_axis=0,...  93.1 us
    all_to_all x1, waiting for transfers between devices, body(): lax.all_to_all(back_send, 'expert', split_axis=0, concat_axis=0, tiled=True)  43.7 us
    dot_general x1, matrix products, body(): lax.dot_general(jnp.stack([row_x, row_x, scaled_grad]), jnp.stack([gate_r...  11.7 us
    unnamed x28, local copies, waits for them, and re-layouts  9.21 us
    all_to_all x1, starting transfers between devices, body(): lax.all_to_all(back_send, 'expert', split_axis=0, concat_axis=0, tiled=True)  6.06 us
    convert_element_type x2, other arithmetic, body(): scaled_grad = (weight * row_g.astype(jnp.float32)).astype(jnp.bfloat16)  4.94 us
    convert_element_type x1, local copies, waits for them, and re-layouts, body(): scaled_grad = (weight * row_g.astype(jnp.float32)).astype(jnp.bfloat16)  4.64 us
  transfers between devices with their start and end apart: 2, of which 1 were waited for; matrix products, arithmetic and copies ran while one was open for 6% of the time, Pallas kernels for 0%

profile of v7, /device:TPU:8, one launch (start us, length us, event | category | flops | bytes accessed | tf_op | source)
XLA Modules:
  0.0 227.8 jit_solution(1975087841548189738)
XLA Ops:
  7.2 0.9 copy.45
  9.9 1.3 fusion.88
  12.6 2.7 %fusion.74 = (bf16[6,8,16,128]{3,1,2,0:T(8,128)(2,1)S(1)}, bf16[6,8,16,128]{3,1,2,0:T(8,128)(2,1)S(1)}) fusion(bf16[48,2048]{1,0:T(8,128)(2,1)} %param.9, s32[]{:T(128)S(6)} %xor.58, s32[48]{0:T(128)S(1)} %add_multiply_fusion, s32[]{:T(128)S(6)} %xor.50, bf16[48,2048]{1,0:T(8,128)(2,1)} %param.8), kind=kLoop, calls=%fused_computation.121 | loop fusion | flops 13074432 | bytes 786632
  19.4 4.3 %gather_fusion = bf16[864,16,128]{2,1,0:T(8,128)(2,1)} fusion(bf16[130,16,128]{2,1,0:T(8,128)(2,1)} %pad_dynamic-update-slice_fusion, s32[1024]{0:T(1024)S(1)} %pad_clamp_fusion), kind=kCustom, calls=%fused_computation | custom fusion | bytes 7081344 | tf_op jit(solution)/shard_map/gather | solution.py:76
  23.7 93.1 %all_to_all.10 = bf16[32,27,16,128]{3,2,1,0:T(8,128)(2,1)S(1)} all-to-all(bf16[32,27,16,128]{3,2,1,0:T(8,128)(2,1)} %bitcast.86), channel_id=1, replica_groups=mesh['dp'=8,'expert'=32] {'expert'}, dimensions={0} | all-to-all | bytes 7077888 | tf_op jit(solution)/shard_map/all_to_all | solution.py:76
  116.8 3.5 %slice_convert_fusion.2 = (f32[32,13,16,128]{3,2,1,0:T(8,128)}, bf16[32,13,16,128]{3,2,1,0:T(8,128)(2,1)}, bf16[32,13,16,128]{3,2,1,0:T(8,128)(2,1)}) fusion(bf16[32,27,16,128]{3,2,1,0:T(8,128)(2,1)S(1)} %all_to_all.10), kind=kLoop, calls=%fused_computation.162 | loop fusion | flops 851968 | bytes 10223616 | tf_op jit(solution)/shard_map/convert_element_type | solution.py:95
  120.6 4.6 %reshape.325 = f32[1,416,2048]{2,1,0:T(8,128)} reshape(f32[32,13,16,128]{3,2,1,0:T(8,128)} %get-tuple-element.35) | data formatting | bytes 6815744 | tf_op jit(solution)/shard_map/convert_element_type | solution.py:95
  126.3 3.8 %stack_reshape.4 = bf16[1,416,2048]{2,1,0:T(8,128)(2,1)} reshape(bf16[32,13,16,128]{3,2,1,0:T(8,128)(2,1)} %get-tuple-element.36) | data formatting | bytes 3407872 | tf_op jit(solution)/shard_map/stack;reshape | solution.py:108
  130.1 4.0 %fusion.12 = f32[416,768]{1,0:T(8,128)S(1)} fusion(bf16[1,2048,768]{2,1,0:T(8,128)(2,1)} %param.13, bf16[52,8,16,128]{3,2,1,0:T(8,128)(2,1)} %bitcast.87), kind=kOutput, calls=%fused_computation.17 | convolution fusion | flops 1308622848 | bytes 6127616 | tf_op jit(solution)/shard_map/dot_general | solution.py:84
  134.1 1.5 fusion.8
  136.1 1.4 multiply_convert_fusion
  138.1 0.9 copy-done.6
  139.1 3.3 %multiply_reduce_fusion = (bf16[416]{0:T(512)(128)(2,1)S(1)}, bf16[416,768]{1,0:T(8,128)(2,1)}, bf16[416,768]{1,0:T(8,128)(2,1)}, bf16[416,768]{1,0:T(8,128)(2,1)}) fusion(f32[416,768]{1,0:T(8,128)S(1)} %fusion.12, f32[416,768]{1,0:T(8,128)S(1)} %fusion.8, f32[416]{0:T(512)S(1)} %reshape.323, bf16[1,768,2048]{2,1,0:T(8,128)(2,1)S(1)} %copy-done.6, ...), kind=kOutput, calls=%fused_computation.37 | convolution fusion | flops 1314692736 | bytes 9324992 | tf_op jit(solution)/shard_map/dot_general | solution.py:88
  142.4 11.7 %convolution_convert_fusion = bf16[3,2048,768]{2,1,0:T(8,128)(2,1)} fusion(bf16[1,416,2048]{2,1,0:T(8,128)(2,1)} %multiply_convert_fusion, bf16[1,416,2048]{2,1,0:T(8,128)(2,1)} %stack_reshape.4, bf16[1,416,768]{2,1,0:T(8,128)(2,1)} %bitcast.96, bf16[1,416,768]{2,1,0:T(8,128)(2,1)} %bitcast.94, bf16[1,416,768]{2,1,0:T(8,128)(2,1)} %bitcast.95), kind=kOutput, calls=%fused_computation.1 | convolution fusion | flops 3937615872 | bytes 14761984 | tf_op jit(solution)/shard_map/dot_general | solution.py:107
  154.2 2.7 %fusion.6 = f32[416,2048]{1,0:T(8,128)S(1)} fusion(bf16[416,768]{1,0:T(8,128)(2,1)} %get-tuple-element.34, bf16[1,2048,768]{2,1,0:T(8,128)(2,1)S(1)} %copy-done), kind=kOutput, calls=%fused_computation.11 | convolution fusion | flops 1308622848 | bytes 7192576 | tf_op jit(solution)/shard_map/dot_general | solution.py:97
  157.0 1.5 fusion.30
  158.5 1.7 copy.61
  160.3 3.0 %fusion.23 = bf16[32,14,16,128]{3,2,1,0:T(8,128)(2,1)} fusion(bf16[32,1,1,13]{3,2,1,0:T(2,128)(2,1)S(1)} %convert_element_type.179, bf16[32,13,16,128]{3,2,1,0:T(8,128)(2,1)} %bitcast.89), kind=kLoop, calls=%fused_computation.27 | loop fusion | flops 5505024 | bytes 3539776 | tf_op jit(solution)/shard_map/concatenate | solution.py:103
  163.3 6.1 %all-to-all-start.1 = ((bf16[32,14,16,128]{3,2,1,0:T(8,128)(2,1)}), bf16[32,14,16,128]{3,2,1,0:T(8,128)(2,1)}, u32[]{:S(2)}, u32[]{:S(2)}) async-start(bf16[32,14,16,128]{3,2,1,0:T(8,128)(2,1)} %fusion.23), calls=%async_computation.1 | async-start | bytes 3670016 | tf_op jit(solution)/shard_map/all_to_all | solution.py:106
  169.6 43.7 %all-to-all-done.1 = bf16[32,14,16,128]{3,2,1,0:T(8,128)(2,1)} async-done(((bf16[32,14,16,128]{3,2,1,0:T(8,128)(2,1)}), bf16[32,14,16,128]{3,2,1,0:T(8,128)(2,1)}, u32[]{:S(2)}, u32[]{:S(2)}) %all-to-all-start.1) | async-done | bytes 1835040 | tf_op jit(solution)/shard_map/all_to_all | solution.py:106
  213.3 0.9 fusion.80
  215.2 2.6 %convolution_convert_fusion.1 = bf16[48,2048]{1,0:T(8,128)(2,1)} fusion(bf16[56,8,16,128]{3,2,1,0:T(8,128)(2,1)} %bitcast.33, s32[448]{0:T(512)S(1)} %select_reduce_fusion), kind=kOutput, calls=%fused_computation.21 | convolution fusion | flops 88200192 | bytes 2033408 | tf_op jit(solution)/shard_map/dot_general | solution.py:120
  217.8 2.2 slice_bitcast_fusion
  220.0 0.9 copy.53
  (58 shorter events, 9.6 us)
Async XLA Ops:
  7.2 126.9 %copy-start = (bf16[1,2048,768]{2,1,0:T(8,128)(2,1)S(1)}, bf16[1,2048,768]{2,1,0:T(8,128)(2,1)}, u32[]{:S(2)}) copy-start(bf16[1,2048,768]{2,1,0:T(8,128)(2,1)} %param.12) | copy-start | bytes 9437188
  7.2 10.7 %copy-start.5 = (f32[48,8]{0,1:T(8,128)S(1)}, f32[48,8]{0,1:T(8,128)}, u32[]{:S(2)}) copy-start(f32[48,8]{0,1:T(8,128)} %param.11) | copy-start | bytes 4612
  7.2 210.6 %reduce-scatter.2.cloned.1.call-start = ((), (), s32[]{:S(2)}) async-start(), calls=%async_computation.3 | async-start | bytes 10616832 | tf_op jit(solution)/shard_map/reduce_scatter | solution.py:113
  116.8 3.8 %copy-start.1 = (bf16[32,27,16,128]{3,2,1,0:T(8,128)(2,1)}, bf16[32,27,16,128]{3,2,1,0:T(8,128)(2,1)S(1)}, u32[]{:S(2)}) copy-start(bf16[32,27,16,128]{3,2,1,0:T(8,128)(2,1)S(1)} %all_to_all.10) | copy-start | bytes 10616836
  130.1 4.0 %copy-start.3 = (bf16[32,13,16,128]{3,2,1,0:T(8,128)(2,1)S(1)}, bf16[32,13,16,128]{3,2,1,0:T(8,128)(2,1)}, u32[]{:S(2)}) copy-start(bf16[32,13,16,128]{3,2,1,0:T(8,128)(2,1)} %get-tuple-element.36) | copy-start | bytes 5111812
  134.1 2.0 copy-start.2
  136.1 2.1 copy-start.4
  136.1 3.0 %copy-start.6 = (bf16[1,768,2048]{2,1,0:T(8,128)(2,1)S(1)}, bf16[1,768,2048]{2,1,0:T(8,128)(2,1)}, u32[]{:S(2)}) copy-start(bf16[1,768,2048]{2,1,0:T(8,128)(2,1)} %param.14) | copy-start | bytes 9437188
  154.2 2.8 %copy-start.7 = (bf16[1,2048,768]{2,1,0:T(8,128)(2,1)S(1)}, bf16[1,2048,768]{2,1,0:T(8,128)(2,1)}, u32[]{:S(2)}) copy-start(bf16[1,2048,768]{2,1,0:T(8,128)(2,1)} %param.13) | copy-start | bytes 9437188
  154.2 2.8 %copy-start.8 = (bf16[416,768]{1,0:T(8,128)(2,1)S(1)}, bf16[416,768]{1,0:T(8,128)(2,1)}, u32[]{:S(2)}) copy-start(bf16[416,768]{1,0:T(8,128)(2,1)} %get-tuple-element.38) | copy-start | bytes 1916932
  163.3 49.9 %all-to-all-start.1 = ((bf16[32,14,16,128]{3,2,1,0:T(8,128)(2,1)}), bf16[32,14,16,128]{3,2,1,0:T(8,128)(2,1)}, u32[]{:S(2)}, u32[]{:S(2)}) async-start(bf16[32,14,16,128]{3,2,1,0:T(8,128)(2,1)} %fusion.23), calls=%async_computation.1 | async-start | bytes 3670016 | tf_op jit(solution)/shard_map/all_to_all | solution.py:106
Sparse Core Ops, SparseCore 0:
  154.3 56.6 reduce-scatter.1

commit v8 on v6

--- a/solution.py
+++ b/solution.py
@@ -37,8 +37,11 @@
     tile_rows = model_width // lanes
     source_block = lax.axis_index("dp") * owners + lax.axis_index("expert")
     tok_index = source_block * tok_dev + jnp.arange(tok_dev, dtype=jnp.int32)
-    x_dith = dither(tokens, tok_index, dither_keys[0])
-    g_dith = dither(grad_out, tok_index, dither_keys[1])
+    both_dith = dither(
+        jnp.concatenate([tokens, grad_out], axis=0),
+        jnp.concatenate([tok_index, tok_index]),
+        jnp.repeat(dither_keys[:2], tok_dev)[:, None],
+    )
     flat_ids = expert_ids.reshape(-1)
     onehot = (flat_ids[:, None] == jnp.arange(owners, dtype=jnp.int32)[None, :]).astype(jnp.int32)
     position = jnp.sum((jnp.cumsum(onehot, axis=0) - 1) * onehot, axis=1)
@@ -54,22 +57,15 @@
         slot_weight.reshape(owners, 1, capacity), ((0, 0), (0, tile_rows - 1), (0, lanes - capacity))
     )
     table = jnp.concatenate(
-        [
-            x_dith.reshape(tok_dev, tile_rows, lanes),
-            empty_tile,
-            g_dith.reshape(tok_dev, tile_rows, lanes),
-            empty_tile,
-            weight_tiles,
-        ],
-        axis=0,
+        [both_dith.reshape(2 * tok_dev, tile_rows, lanes), weight_tiles, empty_tile], axis=0
     )
     rows_by_dest = source_row.reshape(owners, capacity)
-    weight_base = 2 * (tok_dev + 1)
+    empty_index = 2 * tok_dev + owners
     tile_index = jnp.concatenate(
         [
-            rows_by_dest,
-            rows_by_dest + (tok_dev + 1),
-            weight_base + jnp.arange(owners, dtype=jnp.int32)[:, None],
+            jnp.where(rows_by_dest == tok_dev, empty_index, rows_by_dest),
+            jnp.where(rows_by_dest == tok_dev, empty_index, rows_by_dest + tok_dev),
+            2 * tok_dev + jnp.arange(owners, dtype=jnp.int32)[:, None],
         ],
         axis=1,
     )

time: 212 us -> 219 us (1.033)
  other arithmetic: 11.7 us -> 19.7 us
    convert_element_type x0 -> x1, other arithmetic: none -> 3.04 us  [dither(): return jnp.where(values < 0, -rounded, rounded).astype(jnp.bfloat16)]
    unnamed x1 -> x0, other arithmetic: 2.68 us -> none
    unnamed x30 -> x34, local copies, waits for them, and re-layouts: 6.32 us -> 5.65 us
where the time goes in v8:
time: 219 us
  blocking collectives  93.1 us (43%)
  waiting for transfers between devices  43.8 us (20%)
  matrix products  23.2 us (11%)
  other arithmetic  19.7 us (9%)
  local copies, waits for them, and re-layouts  18.4 us (8%)
  between operations  14.3 us (7%)
  starting transfers between devices  6.07 us (3%)
    all_to_all x1, blocking collectives, body(): lax.all_to_all(table[tile_index], 'expert', split_axis=0, concat_axis=0,...  93.1 us
    all_to_all x1, waiting for transfers between devices, body(): lax.all_to_all(back_send, 'expert', split_axis=0, concat_axis=0, tiled=True)  43.8 us
    all_to_all x1, starting transfers between devices, body(): lax.all_to_all(back_send, 'expert', split_axis=0, concat_axis=0, tiled=True)  6.03 us
    unnamed x34, local copies, waits for them, and re-layouts  5.65 us
    dot_general x1, matrix products, body(): back_grad = jnp.dot(row_g, down_w.T, preferred_element_type=jnp.float32)  5.39 us
    another operation x1, other arithmetic, body(): jnp.stack([gate_part.astype(jnp.bfloat16), up_part.astype(jnp.bfloat16),...  4.63 us
  transfers between devices with their start and end apart: 2, of which 1 were waited for; matrix products, arithmetic and copies ran while one was open for 5% of the time, Pallas kernels for 0%

profile of v8, /device:TPU:8, one launch (start us, length us, event | category | flops | bytes accessed | tf_op | source)
XLA Modules:
  0.0 218.7 jit_solution(16297464217003474044)
XLA Ops:
  7.2 0.9 copy.43
  12.5 1.0 copy.56
  13.5 1.0 copy.55
  21.7 3.0 %fusion.56 = bf16[96,16,128]{2,1,0:T(8,128)(2,1)S(1)} fusion(bf16[48,16,128]{2,1,0:T(8,128)(2,1)S(1)} %bitcast.105, bf16[48,16,128]{2,1,0:T(8,128)(2,1)S(1)} %bitcast.106, s32[96]{0:T(128)S(1)} %get-tuple-element.44, s32[16,128]{1,0:T(8,128)} %multiply_add_fusion, s32[96]{0:T(128)S(1)} %get-tuple-element.43), kind=kLoop, calls=%fused_computation.84 | loop fusion | flops 13762560 | bytes 795392 | tf_op jit(solution)/shard_map/convert_element_type | solution.py:27
  24.7 1.7 fusion.58
  26.4 4.3 %gather_fusion = bf16[864,16,128]{2,1,0:T(8,128)(2,1)} fusion(bf16[129,16,128]{2,1,0:T(8,128)(2,1)} %fusion.58, s32[1024]{0:T(1024)S(1)} %pad_clamp_fusion), kind=kCustom, calls=%fused_computation | custom fusion | bytes 7081344 | tf_op jit(solution)/shard_map/gather | solution.py:72
  30.7 93.1 %all_to_all.10 = bf16[32,27,16,128]{3,2,1,0:T(8,128)(2,1)S(1)} all-to-all(bf16[32,27,16,128]{3,2,1,0:T(8,128)(2,1)} %bitcast.97), channel_id=1, replica_groups=mesh['dp'=8,'expert'=32] {'expert'}, dimensions={0} | all-to-all | bytes 7077888 | tf_op jit(solution)/shard_map/all_to_all | solution.py:72
  123.8 1.8 fusion.72
  126.3 2.5 %fusion.7 = f32[416,768]{1,0:T(8,128)} fusion(bf16[1,2048,768]{2,1,0:T(8,128)(2,1)S(1)} %copy-done.9, bf16[52,8,16,128]{3,2,1,0:T(8,128)(2,1)S(1)} %bitcast.99), kind=kOutput, calls=%fused_computation.15 | convolution fusion | flops 1308622848 | bytes 6127616 | tf_op jit(solution)/shard_map/dot_general | solution.py:80
  128.9 2.6 %fusion.3 = f32[416,768]{1,0:T(8,128)} fusion(bf16[1,2048,768]{2,1,0:T(8,128)(2,1)S(1)} %copy-done, bf16[52,8,16,128]{3,2,1,0:T(8,128)(2,1)S(1)} %bitcast.100), kind=kOutput, calls=%fused_computation.11 | convolution fusion | flops 1308622848 | bytes 6127616 | tf_op jit(solution)/shard_map/dot_general | solution.py:79
  131.6 5.4 %multiply_reduce_fusion = (bf16[416]{0:T(512)(128)(2,1)S(1)}, bf16[416,768]{1,0:T(8,128)(2,1)S(1)}, bf16[416,768]{1,0:T(8,128)(2,1)S(1)}, bf16[416,768]{1,0:T(8,128)(2,1)S(1)}) fusion(f32[416,768]{1,0:T(8,128)} %fusion.7, f32[416,768]{1,0:T(8,128)} %fusion.3, f32[416]{0:T(512)S(1)} %reshape.327, bf16[1,768,2048]{2,1,0:T(8,128)(2,1)} %param.14, ...), kind=kOutput, calls=%fused_computation.38 | convolution fusion | flops 1314692736 | bytes 9324992 | tf_op jit(solution)/shard_map/dot_general | solution.py:84
  137.1 2.1 fusion.13
  139.2 1.9 fusion.12
  141.1 1.9 fusion.11
  143.0 4.6 %pad_maximum_fusion = bf16[3,2048,768]{2,1,0:T(8,128)(2,1)} fusion(bf16[1,2048,768]{2,1,0:T(8,128)(2,1)S(1)} %fusion.13, bf16[1,2048,768]{2,1,0:T(8,128)(2,1)S(1)} %fusion.12, bf16[1,2048,768]{2,1,0:T(8,128)(2,1)S(1)} %fusion.11), kind=kLoop, calls=%fused_computation.1 | loop fusion | flops 9437184 | bytes 18874368 | tf_op jit(solution)/shard_map/stack | solution.py:106
  147.8 2.7 %fusion.1 = f32[416,2048]{1,0:T(8,128)S(1)} fusion(bf16[416,768]{1,0:T(8,128)(2,1)} %copy-done.11, bf16[1,2048,768]{2,1,0:T(8,128)(2,1)S(1)} %copy-done), kind=kOutput, calls=%fused_computation.9 | convolution fusion | flops 1308622848 | bytes 7192576 | tf_op jit(solution)/shard_map/dot_general | solution.py:93
  150.5 1.5 fusion.26
  152.5 1.6 fusion.16
  154.1 6.0 %all-to-all-start.1 = ((bf16[32,14,16,128]{3,2,1,0:T(8,128)(2,1)}), bf16[32,14,16,128]{3,2,1,0:T(8,128)(2,1)}, u32[]{:S(2)}, u32[]{:S(2)}) async-start(bf16[32,14,16,128]{3,2,1,0:T(8,128)(2,1)} %fusion.16), calls=%async_computation.1 | async-start | bytes 3670016 | tf_op jit(solution)/shard_map/all_to_all | solution.py:102
  160.4 43.8 %all-to-all-done.1 = bf16[32,14,16,128]{3,2,1,0:T(8,128)(2,1)} async-done(((bf16[32,14,16,128]{3,2,1,0:T(8,128)(2,1)}), bf16[32,14,16,128]{3,2,1,0:T(8,128)(2,1)}, u32[]{:S(2)}, u32[]{:S(2)}) %all-to-all-start.1) | async-done | bytes 1835040 | tf_op jit(solution)/shard_map/all_to_all | solution.py:102
  204.2 0.9 fusion.65
  206.1 2.6 %convolution_convert_fusion.3 = bf16[48,2048]{1,0:T(8,128)(2,1)} fusion(bf16[56,8,16,128]{3,2,1,0:T(8,128)(2,1)} %bitcast.34, s32[448]{0:T(512)S(1)} %select_reduce_fusion), kind=kOutput, calls=%fused_computation.22 | convolution fusion | flops 88200192 | bytes 2033408 | tf_op jit(solution)/shard_map/dot_general | solution.py:116
  208.7 2.2 slice_bitcast_fusion
  210.9 0.9 copy.51
  (68 shorter events, 14.3 us)
Async XLA Ops:
  7.2 121.7 %copy-start = (bf16[1,2048,768]{2,1,0:T(8,128)(2,1)S(1)}, bf16[1,2048,768]{2,1,0:T(8,128)(2,1)}, u32[]{:S(2)}) copy-start(bf16[1,2048,768]{2,1,0:T(8,128)(2,1)} %param.12) | copy-start | bytes 9437188
  7.2 201.5 %reduce-scatter.2.cloned.1.call-start = ((), (), s32[]{:S(2)}) async-start(), calls=%async_computation.3 | async-start | bytes 10616832 | tf_op jit(solution)/shard_map/reduce_scatter | solution.py:109
  11.7 5.4 %copy-start.4 = (s32[384]{0:T(512)}, s32[384]{0:T(512)S(1)}, u32[]{:S(2)}) copy-start(s32[384]{0:T(512)S(1)} %get-tuple-element.31) | copy-start | bytes 4612
  11.7 5.4 %copy-start.6 = (s32[384]{0:T(512)}, s32[384]{0:T(512)S(1)}, u32[]{:S(2)}) copy-start(s32[384]{0:T(512)S(1)} %get-tuple-element.45) | copy-start | bytes 4612
  123.8 2.5 %copy-start.9 = (bf16[1,2048,768]{2,1,0:T(8,128)(2,1)S(1)}, bf16[1,2048,768]{2,1,0:T(8,128)(2,1)}, u32[]{:S(2)}) copy-start(bf16[1,2048,768]{2,1,0:T(8,128)(2,1)} %param.13) | copy-start | bytes 9437188
  125.6 3.3 %copy-start.1 = (bf16[32,13,16,128]{3,2,1,0:T(8,128)(2,1)}, bf16[32,13,16,128]{3,2,1,0:T(8,128)(2,1)S(1)}, u32[]{:S(2)}) copy-start(bf16[32,13,16,128]{3,2,1,0:T(8,128)(2,1)S(1)} %get-tuple-element.35) | copy-start | bytes 5111812
  131.6 5.4 %copy-start.3 = (bf16[32,13,16,128]{3,2,1,0:T(8,128)(2,1)S(1)}, bf16[32,13,16,128]{3,2,1,0:T(8,128)(2,1)}, u32[]{:S(2)}) copy-start(bf16[32,13,16,128]{3,2,1,0:T(8,128)(2,1)} %get-tuple-element.36) | copy-start | bytes 5111812
  137.0 2.2 copy-start.12
  137.0 4.1 %copy-start.11 = (bf16[416,768]{1,0:T(8,128)(2,1)}, bf16[416,768]{1,0:T(8,128)(2,1)S(1)}, u32[]{:S(2)}) copy-start(bf16[416,768]{1,0:T(8,128)(2,1)S(1)} %get-tuple-element.34) | copy-start | bytes 1916932
  137.0 2.1 copy-start.2
  147.7 2.8 %copy-start.10 = (bf16[1,2048,768]{2,1,0:T(8,128)(2,1)S(1)}, bf16[1,2048,768]{2,1,0:T(8,128)(2,1)}, u32[]{:S(2)}) copy-start(bf16[1,2048,768]{2,1,0:T(8,128)(2,1)} %param.13) | copy-start | bytes 9437188
  147.8 2.8 %copy-start.13 = (bf16[416,768]{1,0:T(8,128)(2,1)S(1)}, bf16[416,768]{1,0:T(8,128)(2,1)}, u32[]{:S(2)}) copy-start(bf16[416,768]{1,0:T(8,128)(2,1)} %copy-done.12) | copy-start | bytes 1916932
  154.1 6.1 %copy-start.7 = (s32[384]{0:T(512)S(1)}, s32[384]{0:T(512)}, u32[]{:S(2)}) copy-start(s32[384]{0:T(512)} %copy-done.6) | copy-start | bytes 4612
  154.1 6.1 %copy-start.8 = (s32[384]{0:T(512)S(1)}, s32[384]{0:T(512)}, u32[]{:S(2)}) copy-start(s32[384]{0:T(512)} %get-tuple-element.30) | copy-start | bytes 4612
  154.1 51.1 %copy-start.5 = (s32[384]{0:T(512)S(1)}, s32[384]{0:T(512)}, u32[]{:S(2)}) copy-start(s32[384]{0:T(512)} %copy-done.4) | copy-start | bytes 4612
  154.1 50.1 %all-to-all-start.1 = ((bf16[32,14,16,128]{3,2,1,0:T(8,128)(2,1)}), bf16[32,14,16,128]{3,2,1,0:T(8,128)(2,1)}, u32[]{:S(2)}, u32[]{:S(2)}) async-start(bf16[32,14,16,128]{3,2,1,0:T(8,128)(2,1)} %fusion.16), calls=%async_computation.1 | async-start | bytes 3670016 | tf_op jit(solution)/shard_map/all_to_all | solution.py:102
Sparse Core Ops, SparseCore 0:
  147.8 56.6 reduce-scatter.1
